TPU v7x, 512 devices: a whole 4x8x8 slice. The times are simulated.
512 devices in a mesh: dom: 32 (over x, z), strip: 16 (over y, core).
Axes of the slice: x: 4, y: 8, z: 8, core: 2. Of those that a mesh axis runs over, the one named last changes fastest.
Arguments:
- state: float32 [32, 4, 512, 512], P('dom', None, 'strip'), may hold values from -6 to 6
- copies: int32 [32], replicated, may hold values from 0 to 31
- depth: float32 [512, 512], P('strip'), may hold values from 0.5 to 2
- friction: float32 [512, 512], P('strip'), may hold values from 0.05 to 0.5
- obs_cells: int32 [16, 512], P('strip'), may hold values from 0 to 16383
- obs_values: float32 [16, 512], P('strip'), may hold values from -6 to 6
Outputs:
- forecast: float32 [32, 4, 512, 512], P('dom', None, 'strip')
- log_weights: float32 [32], P('dom')
All inputs are finite; a program needn't handle non-finite values.
Results may differ from a plain program's by a relative error of at most 0.000039.
Values sent between devices are 32-bit elements; how exact they have to be, the bound alone decides.
No kernel may reach another device: no remote copies, remote signals or barrier semaphores. Data moves between devices by JAX's collectives and lax.ppermute only.
A program may use at most 64 MiB of HBM per device.

v0:
```python
import jax
import jax.numpy as jnp
from jax import lax
from jax.sharding import PartitionSpec as P

STEPS = 4


time_step = 0.25
coriolis = 0.3
diffusion = 0.2
obs_variance = 4.0


def padded_2(cells, sides, width):
    for axis, dim in sides:
        count = lax.axis_size(axis)
        ends = count - 1
        head = lax.slice_in_dim(cells, 0, width, axis=dim)
        tail = lax.slice_in_dim(cells, cells.shape[dim] - width, cells.shape[dim], axis=dim)
        cells = jnp.concatenate(
            [
                lax.ppermute(tail, axis, [(i, (i + 1) % count) for i in range(ends)]),
                cells,
                lax.ppermute(head, axis, [((i + 1) % count, i) for i in range(ends)]),
            ],
            axis=dim,
        )
    return cells


def diff_cols(a):
    return (jnp.roll(a, -1, axis=-1) - jnp.roll(a, 1, axis=-1)) * 0.5


def advance(padded, deep, drag, valid):
    eta, velo_u, velo_v, tracer = (padded[:, 0], padded[:, 1], padded[:, 2], padded[:, 3])
    flux_x = deep * velo_u
    flux_y = deep * velo_v
    eta_ext = eta[:, 1:-1] - time_step * (
        diff_cols(flux_x)[:, 1:-1] + (flux_y[:, 2:] - flux_y[:, :-2]) * 0.5
    )
    eta_ext = jnp.where(valid, eta_ext, 0.0)
    eta_new = eta_ext[:, 1:-1]
    inner_u = velo_u[:, 2:-2]
    inner_v = velo_v[:, 2:-2]
    inner_r = drag[2:-2]
    u_new = (
        inner_u
        - time_step * diff_cols(eta_new)
        - time_step * inner_r * inner_u
        + time_step * coriolis * inner_v
    )
    v_new = (
        inner_v
        - time_step * ((eta_ext[:, 2:] - eta_ext[:, :-2]) * 0.5)
        - time_step * inner_r * inner_v
        - time_step * coriolis * inner_u
    )
    inner_c = tracer[:, 2:-2]
    upper = tracer[:, 3:-1]
    lower = tracer[:, 1:-3]
    grad_y = (upper - lower) * 0.5
    laplace = (
        upper
        + lower
        + jnp.roll(inner_c, -1, axis=-1)
        + jnp.roll(inner_c, 1, axis=-1)
        - 4.0 * inner_c
    )
    c_new = (
        inner_c
        - time_step * (inner_u * diff_cols(inner_c) + inner_v * grad_y)
        + time_step * diffusion * laplace
    )
    return jnp.stack([eta_new, u_new, v_new, c_new], axis=1)


def local(state, copies, depth, friction, obs_cells, obs_values):
    per_dev = state.shape[0]
    rows = state.shape[2]
    member_idx = lax.axis_index("dom")
    sources = lax.dynamic_slice_in_dim(copies, member_idx * per_dev, per_dev, 0)
    piece = lax.all_gather(state, "dom", axis=0, tiled=True)
    labels = jnp.arange(piece.shape[0], dtype=jnp.int32)
    hit = labels == sources[0]
    picks = [jnp.sum(jnp.where(hit[:, None, None, None], piece, 0.0), axis=0)]
    member = jnp.stack(picks)
    margin = 2 * STEPS
    statics = padded_2(jnp.stack([depth, friction]), (("strip", 1),), margin)
    strip_idx = lax.axis_index("strip")
    row_all = strip_idx * rows - margin + jnp.arange(rows + 2 * margin, dtype=jnp.int32)
    inside_all = ((row_all >= 0) & (row_all < rows * lax.axis_size("strip")))[:, None]
    for step in range(STEPS):
        padded = padded_2(member, (("strip", 2),), 2)
        offset = margin - 2
        span = rows + 2 * 2
        deep = statics[0, offset : offset + span]
        drag = statics[1, offset : offset + span]
        valid = inside_all[offset + 1 : offset + span - 1]
        kept = inside_all[offset + 2 : offset + span - 2]
        result = advance(padded, deep, drag, valid)
        member = jnp.where(kept[None, None], result, 0.0)
    eta = member[:, 0].reshape(per_dev, -1)
    seen = jnp.take(eta, obs_cells[0], axis=1)
    gap = seen - obs_values[0][None, :]
    partial_value = -jnp.sum(gap * gap, axis=1) * (0.5 / obs_variance)
    summed = lax.psum(partial_value, "strip")
    loglik = lax.all_gather(summed, "dom", axis=0, tiled=True)
    top = jnp.max(loglik)
    total = top + jnp.log(jnp.sum(jnp.exp(loglik - top)))
    mine = lax.dynamic_slice_in_dim(loglik - total, member_idx * per_dev, per_dev, 0)
    return (member, mine)


def solution(mesh):
    placed = (
        P("dom", None, "strip", None),
        P(),
        P("strip", None),
        P("strip", None),
        P("strip", None),
        P("strip", None),
    )
    return jax.shard_map(
        local,
        mesh=mesh,
        in_specs=placed,
        out_specs=(P("dom", None, "strip", None), P("dom")),
        check_vma=False,
    )
```

profile of v0, /device:TPU:32, one launch (start us, length us, event | category | flops | bytes accessed | tf_op | source)
XLA Modules:
  0.0 276.5 jit_solution(14515473599032346318)
XLA Ops:
  7.2 0.7 all-gather.2.cloned.1.call-update
  7.9 0.8 pad_maximum_fusion.24
  8.7 1.9 collective-permute-start.2
  10.6 4.9 %collective-permute-start.3 = (f32[2,8,512]{2,1,0:T(8,128)S(1)}, f32[2,8,512]{2,1,0:T(8,128)S(1)}, u32[]{:S(2)}, u32[]{:S(2)}) collective-permute-start(f32[2,8,512]{2,1,0:T(8,128)S(1)} %get-tuple-element.43), channel_id=1, source_target_pairs={{1,0},{2,1},{3,2},{4,3},{5,4},{6,5},{7,6},{8,7},{9,8},{10,9},{11,1... | collective-permute-start | bytes 98312 | tf_op jit(solution)/shard_map/ppermute | solution.py:25
  15.5 1.2 dynamic_slice.6
  16.7 0.6 iota_compare_fusion
  17.4 102.1 %all-gather.2.cloned.1.call-done = f32[32,4,32,512]{3,2,1,0:T(8,128)} async-done(((f32[1,4,32,512]{3,2,1,0:T(8,128)}), f32[32,4,32,512]{3,2,1,0:T(8,128)}) %all-gather.2.cloned.1.call-update) | async-done | bytes 8388624 | tf_op jit(solution)/shard_map/all_gather | solution.py:84
  119.5 4.6 %select_reduce_fusion = f32[4,32,512]{2,1,0:T(8,128)S(1)} fusion(f32[32,4,32,512]{3,2,1,0:T(8,128)} %all-gather.2.cloned.1.call-done, pred[32]{0:T(512)(128)(4,1)S(1)} %iota_compare_fusion), kind=kLoop, calls=%fused_computation.1 | loop fusion | flops 4128768 | bytes 8650784 | tf_op jit(solution)/shard_map/reduce_sum | solution.py:87
  124.2 1.9 collective-permute-start
  126.1 4.9 %collective-permute-start.1 = (f32[1,4,2,512]{3,2,1,0:T(2,128)S(1)}, f32[1,4,2,512]{3,2,1,0:T(2,128)S(1)}, u32[]{:S(2)}, u32[]{:S(2)}) collective-permute-start(f32[1,4,2,512]{3,2,1,0:T(2,128)S(1)} %get-tuple-element.33), channel_id=1, source_target_pairs={{1,0},{2,1},{3,2},{4,3},{5,4},{6,5},{7,6},{8,7},{9,8},{10,9},{11,1... | collective-permute-start | bytes 49160 | tf_op jit(solution)/shard_map/ppermute | solution.py:25
  131.1 1.3 collective-permute-done.1
  132.5 0.1 fusion.102
  132.7 0.1 fusion.25
  132.8 0.1 fusion.100
  132.9 0.1 fusion.99
  133.0 0.1 fusion.103
  133.1 0.1 fusion.104
  133.1 0.1 fusion.52
  133.2 0.1 add_bitcast_fusion.3
  133.4 0.1 maximum_select_fusion
  133.5 1.9 collective-permute-start.4
  135.4 4.9 %collective-permute-start.5 = (f32[1,4,2,512]{3,2,1,0:T(2,128)S(1)}, f32[1,4,2,512]{3,2,1,0:T(2,128)S(1)}, u32[]{:S(2)}, u32[]{:S(2)}) collective-permute-start(f32[1,4,2,512]{3,2,1,0:T(2,128)S(1)} %get-tuple-element.31), channel_id=1, source_target_pairs={{1,0},{2,1},{3,2},{4,3},{5,4},{6,5},{7,6},{8,7},{9,8},{10,9},{11,1... | collective-permute-start | bytes 49160 | tf_op jit(solution)/shard_map/ppermute | solution.py:25
  140.3 1.4 collective-permute-done.5
  141.8 0.1 fusion.96
  142.0 0.1 fusion.18
  142.1 0.1 fusion.94
  142.2 0.1 fusion.93
  142.2 0.1 fusion.97
  142.3 0.1 fusion.98
  142.4 0.1 fusion.57
  142.5 0.1 add_bitcast_fusion.2
  142.6 0.1 maximum_select_fusion.1
  142.7 1.9 collective-permute-start.6
  144.7 4.9 %collective-permute-start.7 = (f32[1,4,2,512]{3,2,1,0:T(2,128)S(1)}, f32[1,4,2,512]{3,2,1,0:T(2,128)S(1)}, u32[]{:S(2)}, u32[]{:S(2)}) collective-permute-start(f32[1,4,2,512]{3,2,1,0:T(2,128)S(1)} %get-tuple-element.29), channel_id=1, source_target_pairs={{1,0},{2,1},{3,2},{4,3},{5,4},{6,5},{7,6},{8,7},{9,8},{10,9},{11,1... | collective-permute-start | bytes 49160 | tf_op jit(solution)/shard_map/ppermute | solution.py:25
  149.5 1.4 collective-permute-done.7
  151.0 0.1 fusion.90
  151.2 0.1 fusion.11
  151.3 0.1 fusion.88
  151.4 0.1 fusion.87
  151.5 0.1 fusion.91
  151.6 0.1 fusion.92
  151.6 0.1 fusion.62
  151.8 0.1 add_bitcast_fusion.1
  151.9 0.1 maximum_select_fusion.2
  152.0 1.9 collective-permute-start.8
  153.9 4.9 %collective-permute-start.9 = (f32[1,4,2,512]{3,2,1,0:T(2,128)S(1)}, f32[1,4,2,512]{3,2,1,0:T(2,128)S(1)}, u32[]{:S(2)}, u32[]{:S(2)}) collective-permute-start(f32[1,4,2,512]{3,2,1,0:T(2,128)S(1)} %get-tuple-element.27), channel_id=1, source_target_pairs={{1,0},{2,1},{3,2},{4,3},{5,4},{6,5},{7,6},{8,7},{9,8},{10,9},{11,1... | collective-permute-start | bytes 49160 | tf_op jit(solution)/shard_map/ppermute | solution.py:25
  158.8 1.3 dynamic-slice
  160.1 0.1 collective-permute-done.9
  160.3 0.1 fusion.84
  160.5 0.1 fusion.4
  160.6 0.1 fusion.82
  160.7 0.1 fusion.81
  160.7 0.1 fusion.85
  160.9 0.1 fusion.67
  161.0 0.1 add_bitcast_fusion
  161.1 0.1 maximum_select_fusion.3
  161.3 3.1 %gather_fusion = f32[512]{0:T(512)S(1)} fusion(f32[16384]{0:T(1024)S(1)} %bitcast.118, s32[1024]{0:T(1024)S(1)} %pad_clamp_fusion), kind=kCustom, calls=%fused_computation | custom fusion | bytes 6144 | tf_op jit(solution)/shard_map/jit(_take)/gather | solution.py:105
  164.4 0.6 multiply_reduce_fusion
  165.7 27.6 %psum.7 = f32[1]{0:T(128)} all-reduce(f32[1]{0:T(128)} %bitcast.40), channel_id=1, replica_groups=mesh['dom'=32,'strip'=16] {'strip'}, use_global_device_ids=true, to_apply=%region_2.3 | all-reduce | flops 1 | bytes 8 | tf_op jit(solution)/shard_map/psum | solution.py:108
  193.3 1.4 dynamic-update-slice
  194.7 71.2 %all-reduce = f32[32]{0:T(128)S(1)} all-reduce(f32[32]{0:T(128)S(1)} %dynamic-update-slice), channel_id=1, replica_groups=mesh['dom'=32,'strip'=16] {'dom'}, use_global_device_ids=true, to_apply=%add | all-reduce | flops 32 | bytes 256
  265.8 0.6 reduce_max.9
  266.4 1.3 exponential_reduce_fusion
  269.0 0.6 dynamic_slice.7
  (48 shorter events, 1.1 us)
Async XLA Ops:
  7.2 125.3 %copy-start.2 = (f32[32,512]{1,0:T(8,128)S(1)}, f32[32,512]{1,0:T(8,128)}, u32[]{:S(2)}) copy-start(f32[32,512]{1,0:T(8,128)} %param.8) | copy-start | bytes 196612
  7.2 125.3 %copy-start = (f32[32,512]{1,0:T(8,128)S(1)}, f32[32,512]{1,0:T(8,128)}, u32[]{:S(2)}) copy-start(f32[32,512]{1,0:T(8,128)} %param.9) | copy-start | bytes 196612
  7.2 112.3 %all-gather.2.cloned.1.call-start = ((), (), s32[]{:S(2)}) async-start(), calls=%async_computation | async-start | bytes 8650752 | tf_op jit(solution)/shard_map/all_gather | solution.py:84
  8.7 123.7 %collective-permute-start.2 = (f32[2,8,512]{2,1,0:T(8,128)S(1)}, f32[2,8,512]{2,1,0:T(8,128)S(1)}, u32[]{:S(2)}, u32[]{:S(2)}) collective-permute-start(f32[2,8,512]{2,1,0:T(8,128)S(1)} %get-tuple-element.42), channel_id=1, source_target_pairs={{0,1},{1,2},{2,3},{3,4},{4,5},{5,6},{6,7},{7,8},{8,9},{9,10},{10,1... | collective-permute-start | bytes 98312 | tf_op jit(solution)/shard_map/ppermute | solution.py:23
  10.6 121.8 %collective-permute-start.3 = (f32[2,8,512]{2,1,0:T(8,128)S(1)}, f32[2,8,512]{2,1,0:T(8,128)S(1)}, u32[]{:S(2)}, u32[]{:S(2)}) collective-permute-start(f32[2,8,512]{2,1,0:T(8,128)S(1)} %get-tuple-element.43), channel_id=1, source_target_pairs={{1,0},{2,1},{3,2},{4,3},{5,4},{6,5},{7,6},{8,7},{9,8},{10,9},{11,1... | collective-permute-start | bytes 98312 | tf_op jit(solution)/shard_map/ppermute | solution.py:25
  17.4 132.1 %copy-start.3 = (s32[1,512]{1,0:T(1,128)S(1)}, s32[1,512]{1,0:T(1,128)}, u32[]{:S(2)}) copy-start(s32[1,512]{1,0:T(1,128)} %param.10) | copy-start | bytes 6148
  124.2 7.0 %collective-permute-start = (f32[1,4,2,512]{3,2,1,0:T(2,128)S(1)}, f32[1,4,2,512]{3,2,1,0:T(2,128)S(1)}, u32[]{:S(2)}, u32[]{:S(2)}) collective-permute-start(f32[1,4,2,512]{3,2,1,0:T(2,128)S(1)} %get-tuple-element.32), channel_id=1, source_target_pairs={{0,1},{1,2},{2,3},{3,4},{4,5},{5,6},{6,7},{7,8},{8,9},{9,10},{10,1... | collective-permute-start | bytes 49160 | tf_op jit(solution)/shard_map/ppermute | solution.py:23
  126.1 6.3 %collective-permute-start.1 = (f32[1,4,2,512]{3,2,1,0:T(2,128)S(1)}, f32[1,4,2,512]{3,2,1,0:T(2,128)S(1)}, u32[]{:S(2)}, u32[]{:S(2)}) collective-permute-start(f32[1,4,2,512]{3,2,1,0:T(2,128)S(1)} %get-tuple-element.33), channel_id=1, source_target_pairs={{1,0},{2,1},{3,2},{4,3},{5,4},{6,5},{7,6},{8,7},{9,8},{10,9},{11,1... | collective-permute-start | bytes 49160 | tf_op jit(solution)/shard_map/ppermute | solution.py:25
  133.5 6.8 %collective-permute-start.4 = (f32[1,4,2,512]{3,2,1,0:T(2,128)S(1)}, f32[1,4,2,512]{3,2,1,0:T(2,128)S(1)}, u32[]{:S(2)}, u32[]{:S(2)}) collective-permute-start(f32[1,4,2,512]{3,2,1,0:T(2,128)S(1)} %get-tuple-element.30), channel_id=1, source_target_pairs={{0,1},{1,2},{2,3},{3,4},{4,5},{5,6},{6,7},{7,8},{8,9},{9,10},{10,1... | collective-permute-start | bytes 49160 | tf_op jit(solution)/shard_map/ppermute | solution.py:23
  135.4 6.3 %collective-permute-start.5 = (f32[1,4,2,512]{3,2,1,0:T(2,128)S(1)}, f32[1,4,2,512]{3,2,1,0:T(2,128)S(1)}, u32[]{:S(2)}, u32[]{:S(2)}) collective-permute-start(f32[1,4,2,512]{3,2,1,0:T(2,128)S(1)} %get-tuple-element.31), channel_id=1, source_target_pairs={{1,0},{2,1},{3,2},{4,3},{5,4},{6,5},{7,6},{8,7},{9,8},{10,9},{11,1... | collective-permute-start | bytes 49160 | tf_op jit(solution)/shard_map/ppermute | solution.py:25
  141.8 22.6 %copy-start.4 = (f32[1,512]{1,0:T(1,128)S(1)}, f32[1,512]{1,0:T(1,128)}, u32[]{:S(2)}) copy-start(f32[1,512]{1,0:T(1,128)} %param.11) | copy-start | bytes 6148
  142.7 6.8 %collective-permute-start.6 = (f32[1,4,2,512]{3,2,1,0:T(2,128)S(1)}, f32[1,4,2,512]{3,2,1,0:T(2,128)S(1)}, u32[]{:S(2)}, u32[]{:S(2)}) collective-permute-start(f32[1,4,2,512]{3,2,1,0:T(2,128)S(1)} %get-tuple-element.28), channel_id=1, source_target_pairs={{0,1},{1,2},{2,3},{3,4},{4,5},{5,6},{6,7},{7,8},{8,9},{9,10},{10,1... | collective-permute-start | bytes 49160 | tf_op jit(solution)/shard_map/ppermute | solution.py:23
  144.7 6.3 %collective-permute-start.7 = (f32[1,4,2,512]{3,2,1,0:T(2,128)S(1)}, f32[1,4,2,512]{3,2,1,0:T(2,128)S(1)}, u32[]{:S(2)}, u32[]{:S(2)}) collective-permute-start(f32[1,4,2,512]{3,2,1,0:T(2,128)S(1)} %get-tuple-element.29), channel_id=1, source_target_pairs={{1,0},{2,1},{3,2},{4,3},{5,4},{6,5},{7,6},{8,7},{9,8},{10,9},{11,1... | collective-permute-start | bytes 49160 | tf_op jit(solution)/shard_map/ppermute | solution.py:25
  152.0 8.1 %collective-permute-start.8 = (f32[1,4,2,512]{3,2,1,0:T(2,128)S(1)}, f32[1,4,2,512]{3,2,1,0:T(2,128)S(1)}, u32[]{:S(2)}, u32[]{:S(2)}) collective-permute-start(f32[1,4,2,512]{3,2,1,0:T(2,128)S(1)} %get-tuple-element.26), channel_id=1, source_target_pairs={{0,1},{1,2},{2,3},{3,4},{4,5},{5,6},{6,7},{7,8},{8,9},{9,10},{10,1... | collective-permute-start | bytes 49160 | tf_op jit(solution)/shard_map/ppermute | solution.py:23
  153.9 6.3 %collective-permute-start.9 = (f32[1,4,2,512]{3,2,1,0:T(2,128)S(1)}, f32[1,4,2,512]{3,2,1,0:T(2,128)S(1)}, u32[]{:S(2)}, u32[]{:S(2)}) collective-permute-start(f32[1,4,2,512]{3,2,1,0:T(2,128)S(1)} %get-tuple-element.27), channel_id=1, source_target_pairs={{1,0},{2,1},{3,2},{4,3},{5,4},{6,5},{7,6},{8,7},{9,8},{10,9},{11,1... | collective-permute-start | bytes 49160 | tf_op jit(solution)/shard_map/ppermute | solution.py:25
  161.2 108.4 %copy-start.1 = (f32[1,4,32,512]{3,2,1,0:T(8,128)}, f32[1,4,32,512]{3,2,1,0:T(8,128)S(1)}, u32[]{:S(2)}) copy-start(f32[1,4,32,512]{3,2,1,0:T(8,128)S(1)} %maximum_select_fusion.3) | copy-start | bytes 786436
Sparse Core Ops, SparseCore 0:
  11.2 108.3 all-gather.1
where the time goes:
time: 277 us; the launch traced here: 276 us
  waiting for transfers between devices  107 us (39%)
  blocking collectives  98.8 us (36%)
  starting transfers between devices  33.9 us (12%)
  between operations  16.5 us (6%)
  other arithmetic  10.4 us (4%)
  local copies, waits for them, and re-layouts  9.92 us (4%)
    all_gather x1, waiting for transfers between devices, local(): piece = lax.all_gather(state, 'dom', axis=0, tiled=True)  102 us
    unnamed x1, blocking collectives  71.2 us
    psum x1, blocking collectives, local(): summed = lax.psum(partial_value, 'strip')  27.6 us
    ppermute x5, starting transfers between devices, padded_2(): lax.ppermute(head, axis, [((i + 1) % count, i) for i in range(ends)])  24.3 us
    ppermute x5, starting transfers between devices, padded_2(): lax.ppermute(tail, axis, [(i, (i + 1) % count) for i in range(ends)])  9.59 us
  transfers between devices with their start and end apart: 11, of which 5 were waited for; matrix products, arithmetic and copies ran while one was open for 3% of the time, Pallas kernels for 0%

commit v1 on v0

v1 whole, which is shorter than its diff:
```python
import jax
import jax.numpy as jnp
from jax import lax
from jax.sharding import Mesh
from jax.sharding import PartitionSpec as P

STEPS = 4


time_step = 0.25
coriolis = 0.3
diffusion = 0.2
obs_variance = 4.0

DOM = ("dx", "dz")


def diff_cols(a):
    return (jnp.roll(a, -1, axis=-1) - jnp.roll(a, 1, axis=-1)) * 0.5


def advance(padded, deep, drag, valid):
    eta, velo_u, velo_v, tracer = (padded[:, 0], padded[:, 1], padded[:, 2], padded[:, 3])
    flux_x = deep * velo_u
    flux_y = deep * velo_v
    eta_ext = eta[:, 1:-1] - time_step * (
        diff_cols(flux_x)[:, 1:-1] + (flux_y[:, 2:] - flux_y[:, :-2]) * 0.5
    )
    eta_ext = jnp.where(valid, eta_ext, 0.0)
    eta_new = eta_ext[:, 1:-1]
    inner_u = velo_u[:, 2:-2]
    inner_v = velo_v[:, 2:-2]
    inner_r = drag[2:-2]
    u_new = (
        inner_u
        - time_step * diff_cols(eta_new)
        - time_step * inner_r * inner_u
        + time_step * coriolis * inner_v
    )
    v_new = (
        inner_v
        - time_step * ((eta_ext[:, 2:] - eta_ext[:, :-2]) * 0.5)
        - time_step * inner_r * inner_v
        - time_step * coriolis * inner_u
    )
    inner_c = tracer[:, 2:-2]
    upper = tracer[:, 3:-1]
    lower = tracer[:, 1:-3]
    grad_y = (upper - lower) * 0.5
    laplace = (
        upper
        + lower
        + jnp.roll(inner_c, -1, axis=-1)
        + jnp.roll(inner_c, 1, axis=-1)
        - 4.0 * inner_c
    )
    c_new = (
        inner_c
        - time_step * (inner_u * diff_cols(inner_c) + inner_v * grad_y)
        + time_step * diffusion * laplace
    )
    return jnp.stack([eta_new, u_new, v_new, c_new], axis=1)


def halo_frame(cells, width):
    count = lax.axis_size("strip")
    ends = count - 1
    rows = cells.shape[1]
    head = cells[:, :width]
    tail = cells[:, rows - width:]
    above = lax.ppermute(tail, "strip", [(i, i + 1) for i in range(ends)])
    below = lax.ppermute(head, "strip", [(i + 1, i) for i in range(ends)])
    return jnp.concatenate([above, cells, below], axis=1)


def forecast_of(state, depth, friction):
    rows = state.shape[2]
    margin = 2 * STEPS
    packed = jnp.concatenate([state[0], depth[None], friction[None]], axis=0)
    frame = halo_frame(packed, margin)
    member = frame[None, :4]
    deep_all = frame[4]
    drag_all = frame[5]
    strip_idx = lax.axis_index("strip")
    total_rows = rows * lax.axis_size("strip")
    row_all = strip_idx * rows - margin + jnp.arange(rows + 2 * margin, dtype=jnp.int32)
    inside_all = ((row_all >= 0) & (row_all < total_rows))[:, None]
    span = rows + 2 * margin
    for step in range(STEPS):
        lo = 2 * step
        hi = span - 2 * step
        deep = deep_all[lo:hi]
        drag = drag_all[lo:hi]
        valid = inside_all[lo + 1 : hi - 1]
        kept = inside_all[lo + 2 : hi - 2]
        result = advance(member, deep, drag, valid)
        member = jnp.where(kept[None, None], result, 0.0)
    return member


def local(state, copies, depth, friction, obs_cells, obs_values):
    nx = lax.axis_size("dx")
    nz = lax.axis_size("dz")
    n_dom = nx * nz
    mx = lax.axis_index("dx")
    mz = lax.axis_index("dz")
    me = mx * nz + mz

    fore = forecast_of(state, depth, friction)

    eta = fore[0, 0].reshape(-1)
    seen = jnp.take(eta, obs_cells[0], axis=0)
    gap = seen - obs_values[0]
    partial_value = -jnp.sum(gap * gap) * (0.5 / obs_variance)
    slots = jnp.where(jnp.arange(n_dom) == me, partial_value, 0.0)
    by_source = lax.psum(slots, ("dx", "dz", "strip"))

    along_z = lax.all_gather(fore[0], "dz", axis=0, tiled=False)
    dest = jnp.arange(nx) * nz + mz
    src = copies[dest]
    picks = jnp.take(along_z, src % nz, axis=0)
    moved = lax.all_to_all(picks, "dx", 0, 0, tiled=False)
    mine_src = copies[me]
    member = lax.dynamic_index_in_dim(moved, mine_src // nz, axis=0, keepdims=True)

    loglik = by_source[copies]
    top = jnp.max(loglik)
    total = top + jnp.log(jnp.sum(jnp.exp(loglik - top)))
    mine = lax.dynamic_slice_in_dim(loglik - total, me, 1, 0)
    return (member, mine)


def solution(mesh):
    n_dom = mesh.shape["dom"]
    xs = sorted({d.coords[0] for d in mesh.devices[:, 0]})
    nx = len(xs)
    devices = mesh.devices.reshape(nx, n_dom // nx, mesh.shape["strip"])
    split = Mesh(devices, ("dx", "dz", "strip"))
    placed = (
        P(DOM, None, "strip", None),
        P(),
        P("strip", None),
        P("strip", None),
        P("strip", None),
        P("strip", None),
    )
    return jax.shard_map(
        local,
        mesh=split,
        in_specs=placed,
        out_specs=(P(DOM, None, "strip", None), P(DOM)),
        check_vma=False,
    )
```

time: 277 us -> 196 us (0.71)
  the two profiles are of different devices: /device:TPU:32 before, /device:TPU:1 now
where the time goes in v1:
time: 196 us; the launch traced here: 195 us
  blocking collectives  102 us (52%)
  waiting for transfers between devices  40.2 us (21%)
  between operations  19.1 us (10%)
  starting transfers between devices  14.2 us (7%)
  local copies, waits for them, and re-layouts  12.1 us (6%)
  other arithmetic  8.25 us (4%)
    psum x1, blocking collectives, local(): by_source = lax.psum(slots, ('dx', 'dz', 'strip'))  102 us
    all_gather x1, waiting for transfers between devices, local(): along_z = lax.all_gather(fore[0], 'dz', axis=0, tiled=False)  39.9 us
    ppermute x1, starting transfers between devices, halo_frame(): below = lax.ppermute(head, 'strip', [(i + 1, i) for i in range(ends)])  5.46 us
    ppermute x1, starting transfers between devices, halo_frame(): above = lax.ppermute(tail, 'strip', [(i, i + 1) for i in range(ends)])  4.58 us
    all_to_all x1, starting transfers between devices, local(): moved = lax.all_to_all(picks, 'dx', 0, 0, tiled=False)  4.1 us
  transfers between devices with their start and end apart: 4, of which 2 were waited for; matrix products, arithmetic and copies ran while one was open for 5% of the time, Pallas kernels for 0%

profile of v1, /device:TPU:1, one launch (start us, length us, event | category | flops | bytes accessed | tf_op | source)
XLA Modules:
  0.0 195.4 jit_solution(17649033361596573586)
XLA Ops:
  7.2 1.0 pad_maximum_fusion.7
  8.2 4.6 %collective-permute-start = (f32[6,8,512]{2,1,0:T(8,128)S(1)}, f32[6,8,512]{2,1,0:T(8,128)S(1)}, u32[]{:S(2)}, u32[]{:S(2)}) collective-permute-start(f32[6,8,512]{2,1,0:T(8,128)S(1)} %get-tuple-element.24), channel_id=1, source_target_pairs={{0,1},{1,2},{2,3},{3,4},{4,5},{5,6},{6,7},{7,8},{8,9},{9,10},{10,1... | collective-permute-start | bytes 294920 | tf_op jit(solution)/shard_map/ppermute | solution.py:71
  12.8 5.5 %collective-permute-start.1 = (f32[6,8,512]{2,1,0:T(8,128)S(1)}, f32[6,8,512]{2,1,0:T(8,128)S(1)}, u32[]{:S(2)}, u32[]{:S(2)}) collective-permute-start(f32[6,8,512]{2,1,0:T(8,128)S(1)} %get-tuple-element.25), channel_id=1, source_target_pairs={{1,0},{2,1},{3,2},{4,3},{5,4},{6,5},{7,6},{8,7},{9,8},{10,9},{11,1... | collective-permute-start | bytes 294920 | tf_op jit(solution)/shard_map/ppermute | solution.py:72
  18.2 0.1 slice.500
  18.3 0.1 slice.499
  18.5 0.1 slice.497
  18.5 0.1 slice.496
  18.6 0.1 slice.495
  18.7 0.1 slice.494
  18.9 0.3 collective-permute-done.1
  19.1 1.1 pad_maximum_fusion
  20.3 0.1 fusion.81
  20.4 0.1 fusion.80
  20.5 0.1 fusion.16
  20.6 0.1 fusion.79
  20.7 0.1 fusion.78
  20.8 0.1 fusion.82
  20.9 0.1 fusion.83
  21.0 0.1 fusion.23
  21.1 0.1 add_bitcast_fusion
  21.2 0.1 maximum_select_fusion
  21.3 0.1 fusion.75
  21.4 0.1 fusion.74
  21.5 0.1 fusion.4
  21.7 0.1 fusion.73
  21.8 0.1 fusion.72
  21.8 0.1 fusion.76
  21.9 0.1 fusion.77
  22.0 0.1 fusion.52
  22.1 0.1 add_bitcast_fusion.2
  22.2 0.1 maximum_select_fusion.1
  22.4 0.1 fusion.93
  22.5 0.1 fusion.40
  22.7 0.1 fusion.91
  22.8 0.1 fusion.90
  22.8 0.1 fusion.94
  22.9 0.1 fusion.95
  23.0 0.1 fusion.57
  23.1 0.1 add_bitcast_fusion.1
  23.2 0.1 maximum_select_fusion.2
  23.4 0.1 fusion.87
  23.6 0.1 fusion.28
  23.7 0.1 fusion.85
  23.8 0.1 fusion.84
  23.9 0.1 fusion.88
  23.9 0.1 fusion.89
  24.0 0.1 fusion.67
  24.1 0.1 add_bitcast_fusion.3
  24.2 0.8 maximum_select_fusion.3
  25.1 0.6 dynamic_slice.10
  27.6 0.6 gather_fusion
  29.0 39.9 %all-gather.2.cloned.1.call-done = f32[8,4,32,512]{3,2,1,0:T(8,128)} async-done(((f32[1,4,32,512]{3,2,1,0:T(8,128)}), f32[8,4,32,512]{3,2,1,0:T(8,128)}) %all-gather.2.cloned.1.call-update) | async-done | bytes 2097168 | tf_op jit(solution)/shard_map/all_gather | solution.py:118
  69.0 2.2 %gather_fusion.1 = f32[4,4,32,512]{3,2,1,0:T(8,128)S(1)} fusion(f32[8,4,32,512]{3,2,1,0:T(8,128)} %all-gather.2.cloned.1.call-done, s32[1024]{0:T(1024)S(1)} %pad_clamp_fusion.2), kind=kCustom, calls=%fused_computation.1 | custom fusion | bytes 2097168 | tf_op jit(solution)/shard_map/jit(_take)/gather | solution.py:121
  71.2 1.2 broadcast_select_fusion
  72.4 4.1 %all-to-all-start = ((f32[4,4,32,512]{3,2,1,0:T(8,128)}), f32[4,4,32,512]{3,2,1,0:T(8,128)S(1)}, u32[]{:S(2)}, u32[]{:S(2)}) async-start(f32[4,4,32,512]{3,2,1,0:T(8,128)} %broadcast_select_fusion), calls=%async_computation | async-start | bytes 2097152 | tf_op jit(solution)/shard_map/all_to_all | solution.py:122
  76.5 0.8 slice_bitcast_fusion.20
  77.4 3.1 %gather_fusion.2 = f32[512]{0:T(512)S(1)} fusion(f32[16384]{0:T(1024)S(1)} %bitcast.107, s32[1024]{0:T(1024)S(1)} %pad_clamp_fusion.1), kind=kCustom, calls=%fused_computation.2 | custom fusion | bytes 6144 | tf_op jit(solution)/shard_map/jit(_take)/gather | solution.py:112
  80.5 0.6 multiply_reduce_fusion
  81.8 101.5 %psum.7 = f32[32]{0:T(128)S(1)} all-reduce(f32[32]{0:T(128)S(1)} %compare_select_fusion.10), channel_id=1, replica_groups=mesh['dx'=4,'dz'=8,'strip'=16] {'dx','dz','strip'}, use_global_device_ids=true, to_apply=%region_1.2 | all-reduce | flops 32 | bytes 256 | tf_op jit(solution)/shard_map/psum | solution.py:116
  183.3 0.7 gather_fusion.3
  184.0 0.6 reduce_max.9
  184.6 1.2 exponential_reduce_fusion
  187.2 0.6 dynamic_slice.12
  187.8 0.7 constant_dynamic-slice_fusion
  (38 shorter events, 0.7 us)
Async XLA Ops:
  7.2 61.8 %all-gather.2.cloned.1.call-start = ((), (), s32[]{:S(2)}) async-start(), calls=%async_computation.1 | async-start | bytes 2359296 | tf_op jit(solution)/shard_map/all_gather | solution.py:118
  8.2 10.7 %collective-permute-start = (f32[6,8,512]{2,1,0:T(8,128)S(1)}, f32[6,8,512]{2,1,0:T(8,128)S(1)}, u32[]{:S(2)}, u32[]{:S(2)}) collective-permute-start(f32[6,8,512]{2,1,0:T(8,128)S(1)} %get-tuple-element.24), channel_id=1, source_target_pairs={{0,1},{1,2},{2,3},{3,4},{4,5},{5,6},{6,7},{7,8},{8,9},{9,10},{10,1... | collective-permute-start | bytes 294920 | tf_op jit(solution)/shard_map/ppermute | solution.py:71
  12.8 6.4 %collective-permute-start.1 = (f32[6,8,512]{2,1,0:T(8,128)S(1)}, f32[6,8,512]{2,1,0:T(8,128)S(1)}, u32[]{:S(2)}, u32[]{:S(2)}) collective-permute-start(f32[6,8,512]{2,1,0:T(8,128)S(1)} %get-tuple-element.25), channel_id=1, source_target_pairs={{1,0},{2,1},{3,2},{4,3},{5,4},{6,5},{7,6},{8,7},{9,8},{10,9},{11,1... | collective-permute-start | bytes 294920 | tf_op jit(solution)/shard_map/ppermute | solution.py:72
  23.1 0.9 copy-start.1
  23.4 1.6 copy-start
  23.6 5.4 %copy-start.2 = (s32[1,512]{1,0:T(1,128)S(1)}, s32[1,512]{1,0:T(1,128)}, u32[]{:S(2)}) copy-start(s32[1,512]{1,0:T(1,128)} %param.10) | copy-start | bytes 6148
  72.4 8.1 %copy-start.3 = (f32[1,512]{1,0:T(1,128)S(1)}, f32[1,512]{1,0:T(1,128)}, u32[]{:S(2)}) copy-start(f32[1,512]{1,0:T(1,128)} %param.11) | copy-start | bytes 6148
  72.4 115.4 %all-to-all-start = ((f32[4,4,32,512]{3,2,1,0:T(8,128)}), f32[4,4,32,512]{3,2,1,0:T(8,128)S(1)}, u32[]{:S(2)}, u32[]{:S(2)}) async-start(f32[4,4,32,512]{3,2,1,0:T(8,128)} %broadcast_select_fusion), calls=%async_computation | async-start | bytes 2097152 | tf_op jit(solution)/shard_map/all_to_all | solution.py:122
Sparse Core Ops, SparseCore 0:
  25.2 43.7 all-gather.1

commit v2 on v1

--- a/solution.py
+++ b/solution.py
@@ -13,6 +13,9 @@
 obs_variance = 4.0
 
 DOM = ("dx", "dz")
+LOGLIK_MODE = "a2a"
+STAGE1 = "gather"
+STAGE2 = "a2a"
 
 
 def diff_cols(a):
@@ -98,6 +101,16 @@
     return member
 
 
+def butterfly_sum(value, axes):
+    for axis, size in axes:
+        step = 1
+        while step < size:
+            pairs = [(i, i ^ step) for i in range(size)]
+            value = value + lax.ppermute(value, axis, pairs)
+            step *= 2
+    return value
+
+
 def local(state, copies, depth, friction, obs_cells, obs_values):
     nx = lax.axis_size("dx")
     nz = lax.axis_size("dz")
@@ -112,14 +125,39 @@
     seen = jnp.take(eta, obs_cells[0], axis=0)
     gap = seen - obs_values[0]
     partial_value = -jnp.sum(gap * gap) * (0.5 / obs_variance)
-    slots = jnp.where(jnp.arange(n_dom) == me, partial_value, 0.0)
-    by_source = lax.psum(slots, ("dx", "dz", "strip"))
+    if LOGLIK_MODE == "psum":
+        slots = jnp.where(jnp.arange(n_dom) == me, partial_value, 0.0)
+        by_source = lax.psum(slots, ("dx", "dz", "strip"))
+    elif LOGLIK_MODE == "a2a":
+        n_all = n_dom * lax.axis_size("strip")
+        spread = jnp.broadcast_to(partial_value, (n_all, 1))
+        every = lax.all_to_all(spread, ("dx", "dz", "strip"), 0, 0, tiled=True)
+        by_source = jnp.sum(every.reshape(n_dom, -1), axis=1)
+    else:
+        slots = jnp.where(jnp.arange(n_dom) == me, partial_value, 0.0)
+        by_source = butterfly_sum(slots, (("strip", lax.axis_size("strip")), ("dx", nx), ("dz", nz)))
 
-    along_z = lax.all_gather(fore[0], "dz", axis=0, tiled=False)
+    if STAGE1 == "gather":
+        along_z = lax.all_gather(fore[0], "dz", axis=0, tiled=False)
+    else:
+        parts = [None] * nz
+        parts[0] = fore[0]
+        for d in range(1, nz):
+            parts[d] = lax.ppermute(fore[0], "dz", [(i, (i + d) % nz) for i in range(nz)])
+        order = jnp.stack(parts)
+        along_z = jnp.take(order, (mz - jnp.arange(nz)) % nz, axis=0)
     dest = jnp.arange(nx) * nz + mz
     src = copies[dest]
     picks = jnp.take(along_z, src % nz, axis=0)
-    moved = lax.all_to_all(picks, "dx", 0, 0, tiled=False)
+    if STAGE2 == "a2a":
+        moved = lax.all_to_all(picks, "dx", 0, 0, tiled=False)
+    else:
+        got = [None] * nx
+        got[0] = lax.dynamic_index_in_dim(picks, mx, axis=0, keepdims=False)
+        for d in range(1, nx):
+            send = lax.dynamic_index_in_dim(picks, (mx + d) % nx, axis=0, keepdims=False)
+            got[d] = lax.ppermute(send, "dx", [(i, (i + d) % nx) for i in range(nx)])
+        moved = jnp.take(jnp.stack(got), (mx - jnp.arange(nx)) % nx, axis=0)
     mine_src = copies[me]
     member = lax.dynamic_index_in_dim(moved, mine_src // nz, axis=0, keepdims=True)
 

time: 196 us -> 105 us (0.54)
  the two profiles are of different devices: /device:TPU:1 before, /device:TPU:8 now
where the time goes in v2:
time: 105 us
  starting transfers between devices  32.5 us (31%)
  waiting for transfers between devices  30.6 us (29%)
  between operations  19 us (18%)
  local copies, waits for them, and re-layouts  13.1 us (12%)
  other arithmetic  9.36 us (9%)
    all_gather x1, waiting for transfers between devices, local(): along_z = lax.all_gather(fore[0], 'dz', axis=0, tiled=False)  25.7 us
    all_to_all x1, starting transfers between devices, local(): every = lax.all_to_all(spread, ('dx', 'dz', 'strip'), 0, 0, tiled=True)  22.7 us
    all_to_all x1, starting transfers between devices, local(): moved = lax.all_to_all(picks, 'dx', 0, 0, tiled=False)  4.22 us
    ppermute x1, starting transfers between devices, halo_frame(): below = lax.ppermute(head, 'strip', [(i + 1, i) for i in range(ends)])  3.64 us
    all_to_all x1, waiting for transfers between devices, local(): moved = lax.all_to_all(picks, 'dx', 0, 0, tiled=False)  3.26 us
    gather x1, local copies, waits for them, and re-layouts, local(): seen = jnp.take(eta, obs_cells[0], axis=0)  3.14 us
    gather x1, local copies, waits for them, and re-layouts, local(): picks = jnp.take(along_z, src % nz, axis=0)  2.2 us
  transfers between devices with their start and end apart: 5, of which 3 were waited for; matrix products, arithmetic and copies ran while one was open for 14% of the time, Pallas kernels for 0%

profile of v2, /device:TPU:8, one launch (start us, length us, event | category | flops | bytes accessed | tf_op | source)
XLA Modules:
  0.0 104.5 jit_solution(11228465099706247902)
XLA Ops:
  7.2 1.0 pad_maximum_fusion.7
  8.2 1.9 %collective-permute-start = (f32[6,8,512]{2,1,0:T(8,128)S(1)}, f32[6,8,512]{2,1,0:T(8,128)S(1)}, u32[]{:S(2)}, u32[]{:S(2)}) collective-permute-start(f32[6,8,512]{2,1,0:T(8,128)S(1)} %get-tuple-element.24), channel_id=1, source_target_pairs={{0,1},{1,2},{2,3},{3,4},{4,5},{5,6},{6,7},{7,8},{8,9},{9,10},{10,1... | collective-permute-start | bytes 294920 | tf_op jit(solution)/shard_map/ppermute | solution.py:74
  10.1 3.6 %collective-permute-start.1 = (f32[6,8,512]{2,1,0:T(8,128)S(1)}, f32[6,8,512]{2,1,0:T(8,128)S(1)}, u32[]{:S(2)}, u32[]{:S(2)}) collective-permute-start(f32[6,8,512]{2,1,0:T(8,128)S(1)} %get-tuple-element.25), channel_id=1, source_target_pairs={{1,0},{2,1},{3,2},{4,3},{5,4},{6,5},{7,6},{8,7},{9,8},{10,9},{11,1... | collective-permute-start | bytes 294920 | tf_op jit(solution)/shard_map/ppermute | solution.py:75
  13.8 0.1 slice.500
  14.4 1.6 %collective-permute-done.1 = f32[6,8,512]{2,1,0:T(8,128)S(1)} collective-permute-done((f32[6,8,512]{2,1,0:T(8,128)S(1)}, f32[6,8,512]{2,1,0:T(8,128)S(1)}, u32[]{:S(2)}, u32[]{:S(2)}) %collective-permute-start.1) | collective-permute-done | bytes 98336 | tf_op jit(solution)/shard_map/ppermute | solution.py:75
  15.9 1.1 %pad_maximum_fusion = f32[6,48,512]{2,1,0:T(8,128)S(1)} fusion(f32[6,8,512]{2,1,0:T(8,128)S(1)} %collective-permute-done.1, f32[1,32,512]{2,1,0:T(8,128)} %bitcast.111, f32[1,32,512]{2,1,0:T(8,128)} %bitcast.113, f32[4,32,512]{2,1,0:T(8,128)} %bitcast.109, f32[6,8,512]{2,1,0:T(8,128)S(1)} %collective-permute-done), kind=kLoop, calls=%fused_computation.4 | loop fusion | flops 589824 | bytes 1179648 | tf_op jit(solution)/shard_map/concatenate | solution.py:76
  17.1 0.1 fusion.81
  17.2 0.1 fusion.80
  17.3 0.1 fusion.16
  17.4 0.1 fusion.79
  17.5 0.1 fusion.78
  17.6 0.1 fusion.82
  17.7 0.1 fusion.83
  17.8 0.1 fusion.23
  17.9 0.1 add_bitcast_fusion
  18.0 0.1 maximum_select_fusion
  18.1 0.1 fusion.75
  18.2 0.1 fusion.74
  18.3 0.1 fusion.4
  18.4 0.1 fusion.73
  18.5 0.1 fusion.72
  18.6 0.1 fusion.76
  18.7 0.1 fusion.77
  18.8 0.1 fusion.52
  18.9 0.1 add_bitcast_fusion.2
  19.0 0.1 maximum_select_fusion.1
  19.1 0.1 fusion.93
  19.3 0.1 fusion.40
  19.4 0.1 fusion.91
  19.5 0.1 fusion.90
  19.6 0.1 fusion.94
  19.7 0.1 fusion.95
  19.8 0.1 fusion.57
  19.9 0.1 add_bitcast_fusion.1
  20.0 0.1 maximum_select_fusion.2
  20.1 0.1 fusion.87
  20.4 0.1 fusion.28
  20.5 0.1 fusion.85
  20.6 0.1 fusion.84
  20.6 0.1 fusion.88
  20.7 0.1 fusion.89
  20.8 0.1 fusion.67
  20.9 0.1 add_bitcast_fusion.3
  21.0 0.8 maximum_select_fusion.3
  21.9 0.6 gather_fusion
  22.6 0.8 slice_bitcast_fusion.20
  23.5 3.1 %gather_fusion.2 = f32[512]{0:T(512)S(1)} fusion(f32[16384]{0:T(1024)S(1)} %bitcast.107, s32[1024]{0:T(1024)S(1)} %pad_clamp_fusion.1), kind=kCustom, calls=%fused_computation.2 | custom fusion | bytes 6144 | tf_op jit(solution)/shard_map/jit(_take)/gather | solution.py:125
  26.6 0.6 multiply_reduce_fusion
  27.9 0.8 broadcast_in_dim.169
  28.7 22.7 %all-to-all-start.1 = ((f32[512,1,1]{2,1,0:T(1,128)}), f32[512,1,1]{2,1,0:T(1,128)S(1)}, u32[]{:S(2)}, u32[]{:S(2)}) async-start(f32[512,1,1]{2,1,0:T(1,128)} %broadcast_in_dim.169), calls=%async_computation.1 | async-start | bytes 524288 | tf_op jit(solution)/shard_map/all_to_all | solution.py:134
  51.4 25.7 %all-gather.2.cloned.1.call-done = f32[8,4,32,512]{3,2,1,0:T(8,128)} async-done(((f32[1,4,32,512]{3,2,1,0:T(8,128)}), f32[8,4,32,512]{3,2,1,0:T(8,128)}) %all-gather.2.cloned.1.call-update) | async-done | bytes 2097168 | tf_op jit(solution)/shard_map/all_gather | solution.py:141
  77.1 2.2 %gather_fusion.1 = f32[4,4,32,512]{3,2,1,0:T(8,128)S(1)} fusion(f32[8,4,32,512]{3,2,1,0:T(8,128)} %all-gather.2.cloned.1.call-done, s32[1024]{0:T(1024)S(1)} %pad_clamp_fusion.2), kind=kCustom, calls=%fused_computation.1 | custom fusion | bytes 2097168 | tf_op jit(solution)/shard_map/jit(_take)/gather | solution.py:151
  79.3 1.2 %broadcast_select_fusion = f32[4,4,32,512]{3,2,1,0:T(8,128)} fusion(f32[4,4,32,512]{3,2,1,0:T(8,128)S(1)} %gather_fusion.1, pred[4]{0:T(512)(128)(4,1)S(1)} %compare_and_fusion.1), kind=kLoop, calls=%fused_computation.5 | loop fusion | flops 262144 | bytes 2097156 | tf_op jit(solution)/shard_map/jit(_take)/select_n | solution.py:151
  80.5 4.2 %all-to-all-start = ((f32[4,4,32,512]{3,2,1,0:T(8,128)}), f32[4,4,32,512]{3,2,1,0:T(8,128)S(1)}, u32[]{:S(2)}, u32[]{:S(2)}) async-start(f32[4,4,32,512]{3,2,1,0:T(8,128)} %broadcast_select_fusion), calls=%async_computation | async-start | bytes 2097152 | tf_op jit(solution)/shard_map/all_to_all | solution.py:153
  84.7 0.6 dynamic_slice.10
  88.0 1.0 reduce.1
  89.0 0.1 reshape.1095
  89.1 0.1 reduce_sum.28
  89.2 0.7 gather_fusion.3
  89.9 0.6 reduce_max.9
  90.5 1.2 %exponential_reduce_fusion = f32[]{:T(128)} fusion(f32[32]{0:T(128)S(1)} %gather_fusion.3, f32[]{:T(128)} %reduce_max.9), kind=kLoop, calls=%fused_computation.171 | loop fusion | flops 63 | bytes 136 | tf_op jit(solution)/shard_map/reduce_sum | solution.py:166
  93.1 0.6 dynamic_slice.12
  93.7 3.3 %all-to-all-done = f32[4,4,32,512]{3,2,1,0:T(8,128)S(1)} async-done(((f32[4,4,32,512]{3,2,1,0:T(8,128)}), f32[4,4,32,512]{3,2,1,0:T(8,128)S(1)}, u32[]{:S(2)}, u32[]{:S(2)}) %all-to-all-start) | async-done | bytes 1048608 | tf_op jit(solution)/shard_map/all_to_all | solution.py:153
  97.0 0.7 constant_dynamic-slice_fusion
  (42 shorter events, 1.1 us)
Async XLA Ops:
  7.2 70.0 %all-gather.2.cloned.1.call-start = ((), (), s32[]{:S(2)}) async-start(), calls=%async_computation.2 | async-start | bytes 2359296 | tf_op jit(solution)/shard_map/all_gather | solution.py:141
  8.2 6.2 %collective-permute-start = (f32[6,8,512]{2,1,0:T(8,128)S(1)}, f32[6,8,512]{2,1,0:T(8,128)S(1)}, u32[]{:S(2)}, u32[]{:S(2)}) collective-permute-start(f32[6,8,512]{2,1,0:T(8,128)S(1)} %get-tuple-element.24), channel_id=1, source_target_pairs={{0,1},{1,2},{2,3},{3,4},{4,5},{5,6},{6,7},{7,8},{8,9},{9,10},{10,1... | collective-permute-start | bytes 294920 | tf_op jit(solution)/shard_map/ppermute | solution.py:74
  10.1 5.8 %collective-permute-start.1 = (f32[6,8,512]{2,1,0:T(8,128)S(1)}, f32[6,8,512]{2,1,0:T(8,128)S(1)}, u32[]{:S(2)}, u32[]{:S(2)}) collective-permute-start(f32[6,8,512]{2,1,0:T(8,128)S(1)} %get-tuple-element.25), channel_id=1, source_target_pairs={{1,0},{2,1},{3,2},{4,3},{5,4},{6,5},{7,6},{8,7},{9,8},{10,9},{11,1... | collective-permute-start | bytes 294920 | tf_op jit(solution)/shard_map/ppermute | solution.py:75
  19.9 0.9 copy-start.1
  20.2 1.6 %copy-start = (s32[32]{0:T(128)S(1)}, s32[32]{0:T(128)}, u32[]{:S(2)}) copy-start(s32[32]{0:T(128)} %param.7) | copy-start | bytes 388
  20.3 2.2 %copy-start.2 = (s32[1,512]{1,0:T(1,128)S(1)}, s32[1,512]{1,0:T(1,128)}, u32[]{:S(2)}) copy-start(s32[1,512]{1,0:T(1,128)} %param.10) | copy-start | bytes 6148
  20.9 5.7 %copy-start.3 = (f32[1,512]{1,0:T(1,128)S(1)}, f32[1,512]{1,0:T(1,128)}, u32[]{:S(2)}) copy-start(f32[1,512]{1,0:T(1,128)} %param.11) | copy-start | bytes 6148
  28.7 51.8 %all-to-all-start.1 = ((f32[512,1,1]{2,1,0:T(1,128)}), f32[512,1,1]{2,1,0:T(1,128)S(1)}, u32[]{:S(2)}, u32[]{:S(2)}) async-start(f32[512,1,1]{2,1,0:T(1,128)} %broadcast_in_dim.169), calls=%async_computation.1 | async-start | bytes 524288 | tf_op jit(solution)/shard_map/all_to_all | solution.py:134
  80.5 16.4 %all-to-all-start = ((f32[4,4,32,512]{3,2,1,0:T(8,128)}), f32[4,4,32,512]{3,2,1,0:T(8,128)S(1)}, u32[]{:S(2)}, u32[]{:S(2)}) async-start(f32[4,4,32,512]{3,2,1,0:T(8,128)} %broadcast_select_fusion), calls=%async_computation | async-start | bytes 2097152 | tf_op jit(solution)/shard_map/all_to_all | solution.py:153
Sparse Core Ops, SparseCore 0:
  22.0 55.1 all-gather.1

commit v3 on v2

--- a/solution.py
+++ b/solution.py
@@ -148,7 +148,7 @@
         along_z = jnp.take(order, (mz - jnp.arange(nz)) % nz, axis=0)
     dest = jnp.arange(nx) * nz + mz
     src = copies[dest]
-    picks = jnp.take(along_z, src % nz, axis=0)
+    picks = jnp.stack([lax.dynamic_index_in_dim(along_z, src[k] % nz, axis=0, keepdims=False) for k in range(nx)])
     if STAGE2 == "a2a":
         moved = lax.all_to_all(picks, "dx", 0, 0, tiled=False)
     else:

time: 105 us -> 104 us (level)
  waiting for transfers between devices: 30.6 us -> 21.7 us
  between operations: 19 us -> 27 us
    all_gather x1, waiting for transfers between devices: 25.7 us -> 16.6 us  [local(): along_z = lax.all_gather(fore[0], 'dz', axis=0, tiled=False)]
    gather x1 -> x0, local copies, waits for them, and re-layouts: 2.2 us -> none  [local(): picks = jnp.take(along_z, src % nz, axis=0)]
    dynamic_slice x0 -> x1, local copies, waits for them, and re-layouts: none -> 1.27 us  [local(): lax.dynamic_index_in_dim(along_z, src[k] % nz, axis=0, keepdims=False)]
    select_n x2 -> x0, other arithmetic: 1.18 us -> none  [local(): picks = jnp.take(along_z, src % nz, axis=0)]
    another operation x0 -> x1, other arithmetic: none -> 1.07 us  [local(): jnp.stack([lax.dynamic_index_in_dim(along_z, src[k] % nz, axis=0, keepdim...]
where the time goes in v3:
time: 104 us; the launch traced here: 103 us
  starting transfers between devices  32.5 us (31%)
  between operations  27 us (26%)
  waiting for transfers between devices  21.7 us (21%)
  local copies, waits for them, and re-layouts  12.8 us (12%)
  other arithmetic  9.23 us (9%)
    all_to_all x1, starting transfers between devices, local(): every = lax.all_to_all(spread, ('dx', 'dz', 'strip'), 0, 0, tiled=True)  22.7 us
    all_gather x1, waiting for transfers between devices, local(): along_z = lax.all_gather(fore[0], 'dz', axis=0, tiled=False)  16.6 us
    all_to_all x1, starting transfers between devices, local(): moved = lax.all_to_all(picks, 'dx', 0, 0, tiled=False)  4.25 us
    ppermute x1, starting transfers between devices, halo_frame(): below = lax.ppermute(head, 'strip', [(i + 1, i) for i in range(ends)])  3.64 us
    all_to_all x1, waiting for transfers between devices, local(): moved = lax.all_to_all(picks, 'dx', 0, 0, tiled=False)  3.5 us
    gather x1, local copies, waits for them, and re-layouts, local(): seen = jnp.take(eta, obs_cells[0], axis=0)  3.14 us
  transfers between devices with their start and end apart: 5, of which 3 were waited for; matrix products, arithmetic and copies ran while one was open for 14% of the time, Pallas kernels for 0%

profile of v3, /device:TPU:8, one launch (start us, length us, event | category | flops | bytes accessed | tf_op | source)
XLA Modules:
  0.0 103.3 jit_solution(17462462204027024416)
XLA Ops:
  7.2 1.0 pad_maximum_fusion.8
  8.2 1.9 %collective-permute-start = (f32[6,8,512]{2,1,0:T(8,128)S(1)}, f32[6,8,512]{2,1,0:T(8,128)S(1)}, u32[]{:S(2)}, u32[]{:S(2)}) collective-permute-start(f32[6,8,512]{2,1,0:T(8,128)S(1)} %get-tuple-element.28), channel_id=1, source_target_pairs={{0,1},{1,2},{2,3},{3,4},{4,5},{5,6},{6,7},{7,8},{8,9},{9,10},{10,1... | collective-permute-start | bytes 294920 | tf_op jit(solution)/shard_map/ppermute | solution.py:74
  10.1 3.6 %collective-permute-start.1 = (f32[6,8,512]{2,1,0:T(8,128)S(1)}, f32[6,8,512]{2,1,0:T(8,128)S(1)}, u32[]{:S(2)}, u32[]{:S(2)}) collective-permute-start(f32[6,8,512]{2,1,0:T(8,128)S(1)} %get-tuple-element.29), channel_id=1, source_target_pairs={{1,0},{2,1},{3,2},{4,3},{5,4},{6,5},{7,6},{8,7},{9,8},{10,9},{11,1... | collective-permute-start | bytes 294920 | tf_op jit(solution)/shard_map/ppermute | solution.py:75
  13.8 0.1 slice.512
  14.4 1.6 %collective-permute-done.1 = f32[6,8,512]{2,1,0:T(8,128)S(1)} collective-permute-done((f32[6,8,512]{2,1,0:T(8,128)S(1)}, f32[6,8,512]{2,1,0:T(8,128)S(1)}, u32[]{:S(2)}, u32[]{:S(2)}) %collective-permute-start.1) | collective-permute-done | bytes 98336 | tf_op jit(solution)/shard_map/ppermute | solution.py:75
  15.9 1.1 %pad_maximum_fusion.1 = f32[6,48,512]{2,1,0:T(8,128)S(1)} fusion(f32[6,8,512]{2,1,0:T(8,128)S(1)} %collective-permute-done.1, f32[1,32,512]{2,1,0:T(8,128)} %bitcast.111, f32[1,32,512]{2,1,0:T(8,128)} %bitcast.113, f32[4,32,512]{2,1,0:T(8,128)} %bitcast.109, f32[6,8,512]{2,1,0:T(8,128)S(1)} %collective-permute-done), kind=kLoop, calls=%fused_computation.4 | loop fusion | flops 589824 | bytes 1179648 | tf_op jit(solution)/shard_map/concatenate | solution.py:76
  17.1 0.1 fusion.78
  17.2 0.1 fusion.77
  17.3 0.1 fusion.16
  17.4 0.1 fusion.76
  17.5 0.1 fusion.75
  17.6 0.1 fusion.79
  17.7 0.1 fusion.80
  17.8 0.1 fusion.23
  17.9 0.1 add_bitcast_fusion
  18.0 0.1 maximum_select_fusion
  18.1 0.1 fusion.72
  18.3 0.1 fusion.4
  18.4 0.1 fusion.70
  18.5 0.1 fusion.69
  18.6 0.1 fusion.73
  18.7 0.1 fusion.74
  18.8 0.1 fusion.52
  18.9 0.1 add_bitcast_fusion.2
  19.0 0.1 maximum_select_fusion.1
  19.1 0.1 fusion.90
  19.3 0.1 fusion.40
  19.4 0.1 fusion.88
  19.5 0.1 fusion.87
  19.6 0.1 fusion.91
  19.7 0.1 fusion.92
  19.8 0.1 fusion.57
  19.9 0.1 add_bitcast_fusion.1
  20.0 0.1 maximum_select_fusion.2
  20.1 0.1 fusion.84
  20.4 0.1 fusion.28
  20.5 0.1 fusion.82
  20.6 0.1 fusion.81
  20.6 0.1 fusion.85
  20.7 0.1 fusion.86
  20.8 0.1 fusion.67
  20.9 0.1 add_bitcast_fusion.3
  21.0 0.8 maximum_select_fusion.3
  21.9 0.6 gather_fusion
  22.5 0.7 fusion.93
  31.2 0.8 slice_bitcast_fusion.20
  32.1 3.1 %gather_fusion.1 = f32[512]{0:T(512)S(1)} fusion(f32[16384]{0:T(1024)S(1)} %bitcast.107, s32[1024]{0:T(1024)S(1)} %pad_clamp_fusion.1), kind=kCustom, calls=%fused_computation.1 | custom fusion | bytes 6144 | tf_op jit(solution)/shard_map/jit(_take)/gather | solution.py:125
  35.3 0.6 multiply_reduce_fusion
  36.5 0.8 broadcast_in_dim.157
  37.4 22.7 %all-to-all-start.1 = ((f32[512,1,1]{2,1,0:T(1,128)}), f32[512,1,1]{2,1,0:T(1,128)S(1)}, u32[]{:S(2)}, u32[]{:S(2)}) async-start(f32[512,1,1]{2,1,0:T(1,128)} %broadcast_in_dim.157), calls=%async_computation.1 | async-start | bytes 524288 | tf_op jit(solution)/shard_map/all_to_all | solution.py:134
  60.0 16.6 %all-gather.2.cloned.1.call-done = f32[8,4,32,512]{3,2,1,0:T(8,128)} async-done(((f32[1,4,32,512]{3,2,1,0:T(8,128)}), f32[8,4,32,512]{3,2,1,0:T(8,128)}) %all-gather.2.cloned.1.call-update) | async-done | bytes 2097168 | tf_op jit(solution)/shard_map/all_gather | solution.py:141
  76.7 1.3 %constant_dynamic-slice_fusion.4 = (f32[1,4,32,512]{3,2,1,0:T(8,128)S(1)}, f32[1,4,32,512]{3,2,1,0:T(8,128)S(1)}, f32[1,4,32,512]{3,2,1,0:T(8,128)S(1)}, f32[1,4,32,512]{3,2,1,0:T(8,128)S(1)}) fusion(f32[8,4,32,512]{3,2,1,0:T(8,128)} %all-gather.2.cloned.1.call-done, s32[]{:T(128)S(6)} %select_n.151, s32[]{:T(128)S(6)} %select_n.157, s32[]{:T(128)S(6)} %select_n.155, ...), kind=kLoop, calls=%fused_computation.160 | loop fusion | bytes 2097168 | tf_op jit(solution)/shard_map/jit(dynamic_index_in_dim)/dynamic_slice | solution.py:151
  77.9 1.1 %pad_maximum_fusion = f32[4,4,32,512]{3,2,1,0:T(8,128)} fusion(f32[1,4,32,512]{3,2,1,0:T(8,128)S(1)} %get-tuple-element.3, f32[1,4,32,512]{3,2,1,0:T(8,128)S(1)} %get-tuple-element.4, f32[1,4,32,512]{3,2,1,0:T(8,128)S(1)} %get-tuple-element.5, f32[1,4,32,512]{3,2,1,0:T(8,128)S(1)} %get-tuple-element.2), kind=kLoop, calls=%fused_computation.3 | loop fusion | flops 786432 | bytes 2097152 | tf_op jit(solution)/shard_map/stack | solution.py:151
  79.0 4.2 %all-to-all-start = ((f32[4,4,32,512]{3,2,1,0:T(8,128)}), f32[4,4,32,512]{3,2,1,0:T(8,128)S(1)}, u32[]{:S(2)}, u32[]{:S(2)}) async-start(f32[4,4,32,512]{3,2,1,0:T(8,128)} %pad_maximum_fusion), calls=%async_computation | async-start | bytes 2097152 | tf_op jit(solution)/shard_map/all_to_all | solution.py:153
  83.3 0.6 dynamic_slice.27
  86.5 1.0 %reduce.1 = f32[512]{0:T(512)S(1)} reduce(f32[512,1,1]{2,1,0:T(1,128)S(1)} %all-to-all-done.1, f32[]{:T(128)} %constant.150), dimensions={1,2}, to_apply=%all_to_all.8.reduce_sub_computation | reduce | bytes 4100 | tf_op jit(solution)/shard_map/all_to_all | solution.py:134
  87.5 0.1 reshape.1044
  87.6 0.1 reduce_sum.28
  87.7 0.7 gather_fusion.2
  88.4 0.6 reduce_max.9
  89.0 1.2 %exponential_reduce_fusion = f32[]{:T(128)} fusion(f32[32]{0:T(128)S(1)} %gather_fusion.2, f32[]{:T(128)} %reduce_max.9), kind=kLoop, calls=%fused_computation.162 | loop fusion | flops 63 | bytes 136 | tf_op jit(solution)/shard_map/reduce_sum | solution.py:166
  91.6 0.6 dynamic_slice.29
  92.2 3.5 %all-to-all-done = f32[4,4,32,512]{3,2,1,0:T(8,128)S(1)} async-done(((f32[4,4,32,512]{3,2,1,0:T(8,128)}), f32[4,4,32,512]{3,2,1,0:T(8,128)S(1)}, u32[]{:S(2)}, u32[]{:S(2)}) %all-to-all-start) | async-done | bytes 1048608 | tf_op jit(solution)/shard_map/all_to_all | solution.py:153
  95.7 0.7 constant_dynamic-slice_fusion
  (40 shorter events, 1.1 us)
Async XLA Ops:
  7.2 69.5 %all-gather.2.cloned.1.call-start = ((), (), s32[]{:S(2)}) async-start(), calls=%async_computation.2 | async-start | bytes 2359296 | tf_op jit(solution)/shard_map/all_gather | solution.py:141
  8.2 6.2 %collective-permute-start = (f32[6,8,512]{2,1,0:T(8,128)S(1)}, f32[6,8,512]{2,1,0:T(8,128)S(1)}, u32[]{:S(2)}, u32[]{:S(2)}) collective-permute-start(f32[6,8,512]{2,1,0:T(8,128)S(1)} %get-tuple-element.28), channel_id=1, source_target_pairs={{0,1},{1,2},{2,3},{3,4},{4,5},{5,6},{6,7},{7,8},{8,9},{9,10},{10,1... | collective-permute-start | bytes 294920 | tf_op jit(solution)/shard_map/ppermute | solution.py:74
  10.1 5.8 %collective-permute-start.1 = (f32[6,8,512]{2,1,0:T(8,128)S(1)}, f32[6,8,512]{2,1,0:T(8,128)S(1)}, u32[]{:S(2)}, u32[]{:S(2)}) collective-permute-start(f32[6,8,512]{2,1,0:T(8,128)S(1)} %get-tuple-element.29), channel_id=1, source_target_pairs={{1,0},{2,1},{3,2},{4,3},{5,4},{6,5},{7,6},{8,7},{9,8},{10,9},{11,1... | collective-permute-start | bytes 294920 | tf_op jit(solution)/shard_map/ppermute | solution.py:75
  19.9 0.9 copy-start.1
  20.2 1.6 %copy-start = (s32[32]{0:T(128)S(1)}, s32[32]{0:T(128)}, u32[]{:S(2)}) copy-start(s32[32]{0:T(128)} %param.7) | copy-start | bytes 388
  20.4 10.8 %copy-start.2 = (s32[1,512]{1,0:T(1,128)S(1)}, s32[1,512]{1,0:T(1,128)}, u32[]{:S(2)}) copy-start(s32[1,512]{1,0:T(1,128)} %param.10) | copy-start | bytes 6148
  20.9 14.3 %copy-start.3 = (f32[1,512]{1,0:T(1,128)S(1)}, f32[1,512]{1,0:T(1,128)}, u32[]{:S(2)}) copy-start(f32[1,512]{1,0:T(1,128)} %param.11) | copy-start | bytes 6148
  37.4 41.7 %all-to-all-start.1 = ((f32[512,1,1]{2,1,0:T(1,128)}), f32[512,1,1]{2,1,0:T(1,128)S(1)}, u32[]{:S(2)}, u32[]{:S(2)}) async-start(f32[512,1,1]{2,1,0:T(1,128)} %broadcast_in_dim.157), calls=%async_computation.1 | async-start | bytes 524288 | tf_op jit(solution)/shard_map/all_to_all | solution.py:134
  79.0 16.7 %all-to-all-start = ((f32[4,4,32,512]{3,2,1,0:T(8,128)}), f32[4,4,32,512]{3,2,1,0:T(8,128)S(1)}, u32[]{:S(2)}, u32[]{:S(2)}) async-start(f32[4,4,32,512]{3,2,1,0:T(8,128)} %pad_maximum_fusion), calls=%async_computation | async-start | bytes 2097152 | tf_op jit(solution)/shard_map/all_to_all | solution.py:153
Sparse Core Ops, SparseCore 0:
  22.0 54.6 all-gather.1

commit v4 on v3

--- a/solution.py
+++ b/solution.py
@@ -1,7 +1,11 @@
+import functools
+
 import jax
 import jax.numpy as jnp
 from jax import lax
 from jax.sharding import Mesh
+from jax.experimental import pallas as pl
+from jax.experimental.pallas import tpu as pltpu
 from jax.sharding import PartitionSpec as P
 
 STEPS = 4
@@ -76,29 +80,91 @@
     return jnp.concatenate([above, cells, below], axis=1)
 
 
+def _steps_kernel(total_rows, base_ref, state_ref, deep_ref, drag_ref, above_ref, below_ref, out_ref):
+    def frame(k, own):
+        return jnp.concatenate([above_ref[k], own, below_ref[k]], axis=0)
+
+    eta = frame(0, state_ref[0])
+    velo_u = frame(1, state_ref[1])
+    velo_v = frame(2, state_ref[2])
+    tracer = frame(3, state_ref[3])
+    deep = frame(4, deep_ref[...])
+    drag = frame(5, drag_ref[...])
+    rows, cols = eta.shape
+    row = base_ref[0] + lax.broadcasted_iota(jnp.int32, (rows, cols), 0)
+    inside = (row >= 0) & (row < total_rows)
+
+    def east(a):
+        return pltpu.roll(a, cols - 1, 1)
+
+    def west(a):
+        return pltpu.roll(a, 1, 1)
+
+    def north(a):
+        return pltpu.roll(a, rows - 1, 0)
+
+    def south(a):
+        return pltpu.roll(a, 1, 0)
+
+    def dcols(a):
+        return (east(a) - west(a)) * 0.5
+
+    for _ in range(STEPS):
+        flux_x = deep * velo_u
+        flux_y = deep * velo_v
+        eta_new = eta - time_step * (dcols(flux_x) + (north(flux_y) - south(flux_y)) * 0.5)
+        eta_new = jnp.where(inside, eta_new, 0.0)
+        u_new = (
+            velo_u
+            - time_step * dcols(eta_new)
+            - time_step * drag * velo_u
+            + time_step * coriolis * velo_v
+        )
+        v_new = (
+            velo_v
+            - time_step * ((north(eta_new) - south(eta_new)) * 0.5)
+            - time_step * drag * velo_v
+            - time_step * coriolis * velo_u
+        )
+        upper = north(tracer)
+        lower = south(tracer)
+        grad_y = (upper - lower) * 0.5
+        laplace = upper + lower + east(tracer) + west(tracer) - 4.0 * tracer
+        c_new = (
+            tracer
+            - time_step * (velo_u * dcols(tracer) + velo_v * grad_y)
+            + time_step * diffusion * laplace
+        )
+        eta = eta_new
+        velo_u = jnp.where(inside, u_new, 0.0)
+        velo_v = jnp.where(inside, v_new, 0.0)
+        tracer = jnp.where(inside, c_new, 0.0)
+    margin = 2 * STEPS
+    own = rows - 2 * margin
+    out_ref[0, 0] = eta[margin : margin + own]
+    out_ref[0, 1] = velo_u[margin : margin + own]
+    out_ref[0, 2] = velo_v[margin : margin + own]
+    out_ref[0, 3] = tracer[margin : margin + own]
+
+
 def forecast_of(state, depth, friction):
     rows = state.shape[2]
+    cols = state.shape[3]
     margin = 2 * STEPS
+    count = lax.axis_size("strip")
+    ends = count - 1
     packed = jnp.concatenate([state[0], depth[None], friction[None]], axis=0)
-    frame = halo_frame(packed, margin)
-    member = frame[None, :4]
-    deep_all = frame[4]
-    drag_all = frame[5]
-    strip_idx = lax.axis_index("strip")
-    total_rows = rows * lax.axis_size("strip")
-    row_all = strip_idx * rows - margin + jnp.arange(rows + 2 * margin, dtype=jnp.int32)
-    inside_all = ((row_all >= 0) & (row_all < total_rows))[:, None]
-    span = rows + 2 * margin
-    for step in range(STEPS):
-        lo = 2 * step
-        hi = span - 2 * step
-        deep = deep_all[lo:hi]
-        drag = drag_all[lo:hi]
-        valid = inside_all[lo + 1 : hi - 1]
-        kept = inside_all[lo + 2 : hi - 2]
-        result = advance(member, deep, drag, valid)
-        member = jnp.where(kept[None, None], result, 0.0)
-    return member
+    above = lax.ppermute(packed[:, rows - margin:], "strip", [(i, i + 1) for i in range(ends)])
+    below = lax.ppermute(packed[:, :margin], "strip", [(i + 1, i) for i in range(ends)])
+    base = (lax.axis_index("strip") * rows - margin).astype(jnp.int32).reshape(1)
+    vmem = pl.BlockSpec(memory_space=pltpu.VMEM)
+    smem = pl.BlockSpec(memory_space=pltpu.SMEM)
+    return pl.pallas_call(
+        functools.partial(_steps_kernel, rows * count),
+        out_shape=jax.ShapeDtypeStruct(state.shape, state.dtype),
+        in_specs=[smem] + [vmem] * 5,
+        out_specs=vmem,
+    )(base, state[0], depth, friction, above, below)
 
 
 def butterfly_sum(value, axes):

time: 104 us -> 102 us (0.981)
  other arithmetic: 9.23 us -> 5.68 us
  Pallas kernels: 0 us -> 2.92 us
  local copies, waits for them, and re-layouts: 12.8 us -> 10.8 us
  waiting for transfers between devices: 21.7 us -> 23.1 us
    pallas_call x0 -> x1, Pallas kernels: none -> 2.92 us  [forecast_of(): pl.pallas_call(functools.partial(_steps_kernel, rows * count), out_shape=...]
    slice x32 -> x0, local copies, waits for them, and re-layouts: 2.53 us -> none  [the longest x24 1.93 us: diff_cols(): return (jnp.roll(a, -1, axis=-1) - jnp.roll(a, 1, axis=-1)) * 0.5]
    select_n x8 -> x0, other arithmetic: 1.51 us -> none  [the longest x4 1.08 us: forecast_of(): member = jnp.where(kept[None, None], result, 0.0)]
  transfers between devices with their start and end apart: 5 -> 5, of which waited for: 3 -> 4; matrix products, arithmetic and copies ran while one was open for 14% -> 14% of each run, Pallas kernels for 0% -> 0%
where the time goes in v4:
time: 102 us; the launch traced here: 101 us
  starting transfers between devices  32.5 us (32%)
  between operations  26.2 us (26%)
  waiting for transfers between devices  23.1 us (23%)
  local copies, waits for them, and re-layouts  10.8 us (11%)
  other arithmetic  5.68 us (6%)
  Pallas kernels  2.92 us (3%)
    all_to_all x1, starting transfers between devices, local(): every = lax.all_to_all(spread, ('dx', 'dz', 'strip'), 0, 0, tiled=True)  22.7 us
    all_gather x1, waiting for transfers between devices, local(): along_z = lax.all_gather(fore[0], 'dz', axis=0, tiled=False)  17.4 us
    all_to_all x1, starting transfers between devices, local(): moved = lax.all_to_all(picks, 'dx', 0, 0, tiled=False)  4.26 us
    ppermute x1, starting transfers between devices, forecast_of(): lax.ppermute(packed[:, :margin], 'strip', [(i + 1, i) for i in range(ends)])  3.64 us
    all_to_all x1, waiting for transfers between devices, local(): moved = lax.all_to_all(picks, 'dx', 0, 0, tiled=False)  3.46 us
    gather x1, local copies, waits for them, and re-layouts, local(): seen = jnp.take(eta, obs_cells[0], axis=0)  3.14 us
    pallas_call x1, Pallas kernels, forecast_of(): pl.pallas_call(functools.partial(_steps_kernel, rows * count), out_shape=...  2.92 us
  transfers between devices with their start and end apart: 5, of which 4 were waited for; matrix products, arithmetic and copies ran while one was open for 14% of the time, Pallas kernels for 0%

profile of v4, /device:TPU:8, one launch (start us, length us, event | category | flops | bytes accessed | tf_op | source)
XLA Modules:
  0.0 101.1 jit_solution(11260465714512414068)
XLA Ops:
  7.2 0.0 copy-start
  7.2 0.0 copy-start.3
  7.2 0.0 all-gather.2.cloned.1.call-start
  7.2 1.0 pad_maximum_fusion.1
  8.2 0.0 copy-start.4
  8.2 1.9 %collective-permute-start = (f32[6,8,512]{2,1,0:T(8,128)S(1)}, f32[6,8,512]{2,1,0:T(8,128)S(1)}, u32[]{:S(2)}, u32[]{:S(2)}) collective-permute-start(f32[6,8,512]{2,1,0:T(8,128)S(1)} %get-tuple-element.7), channel_id=1, source_target_pairs={{0,1},{1,2},{2,3},{3,4},{4,5},{5,6},{6,7},{7,8},{8,9},{9,10},{10,1... | collective-permute-start | bytes 294920 | tf_op jit(solution)/shard_map/ppermute | solution.py:157
  10.1 3.6 %collective-permute-start.1 = (f32[6,8,512]{2,1,0:T(8,128)S(1)}, f32[6,8,512]{2,1,0:T(8,128)S(1)}, u32[]{:S(2)}, u32[]{:S(2)}) collective-permute-start(f32[6,8,512]{2,1,0:T(8,128)S(1)} %get-tuple-element.6), channel_id=1, source_target_pairs={{1,0},{2,1},{3,2},{4,3},{5,4},{6,5},{7,6},{8,7},{9,8},{10,9},{11,1... | collective-permute-start | bytes 294920 | tf_op jit(solution)/shard_map/ppermute | solution.py:158
  13.8 0.4 collective-permute-done.above_ref
  14.1 0.0 copy-start.1
  14.1 1.8 %collective-permute-done.1.below_ref = f32[6,8,512]{2,1,0:T(8,128)S(1)} collective-permute-done((f32[6,8,512]{2,1,0:T(8,128)S(1)}, f32[6,8,512]{2,1,0:T(8,128)S(1)}, u32[]{:S(2)}, u32[]{:S(2)}) %collective-permute-start.1) | collective-permute-done | bytes 98336 | tf_op jit(solution)/shard_map/ppermute | solution.py:158
  16.0 0.0 copy-start.2
  16.0 0.0 copy-done.1
  16.0 0.6 copy-done.2
  16.6 2.9 %shard_map.77 = f32[1,4,32,512]{3,2,1,0:T(8,128)} custom-call(s32[1]{0:T(128)} %bitcast.base_ref, f32[4,32,512]{2,1,0:T(8,128)} %bitcast.21, f32[32,512]{1,0:T(8,128)} %deep_ref.1, f32[32,512]{1,0:T(8,128)} %drag_ref.1, f32[6,8,512]{2,1,0:T(8,128)} %copy-done.1, f32[6,8,512]{2,1,0:T(8,128)} %copy-done.2), custom_call_target="tpu_custom_call" | custom-call | tf_op jit(solution)/shard_map/pallas_call | solution.py:162
  19.5 0.0 all-gather.2.cloned.1.call-update
  19.6 0.0 copy-done
  19.6 0.6 gather_fusion
  20.2 0.6 fusion.1
  28.3 0.0 copy-done.3
  28.3 0.8 slice_bitcast_fusion
  29.2 3.1 %gather_fusion.1 = f32[512]{0:T(512)S(1)} fusion(f32[16384]{0:T(1024)S(1)} %bitcast.19, s32[1024]{0:T(1024)S(1)} %pad_clamp_fusion.1), kind=kCustom, calls=%fused_computation.1 | custom fusion | bytes 6144 | tf_op jit(solution)/shard_map/jit(_take)/gather | solution.py:191
  32.3 0.0 copy-done.4
  32.3 0.6 multiply_reduce_fusion
  33.6 0.9 broadcast_in_dim.22
  34.4 22.7 %all-to-all-start.1 = ((f32[512,1,1]{2,1,0:T(1,128)}), f32[512,1,1]{2,1,0:T(1,128)S(1)}, u32[]{:S(2)}, u32[]{:S(2)}) async-start(f32[512,1,1]{2,1,0:T(1,128)} %broadcast_in_dim.22), calls=%async_computation.1 | async-start | bytes 524288 | tf_op jit(solution)/shard_map/all_to_all | solution.py:200
  57.1 17.4 %all-gather.2.cloned.1.call-done = f32[8,4,32,512]{3,2,1,0:T(8,128)} async-done(((f32[1,4,32,512]{3,2,1,0:T(8,128)}), f32[8,4,32,512]{3,2,1,0:T(8,128)}) %all-gather.2.cloned.1.call-update) | async-done | bytes 2097168 | tf_op jit(solution)/shard_map/all_gather | solution.py:207
  74.5 1.3 %constant_dynamic-slice_fusion.4 = (f32[1,4,32,512]{3,2,1,0:T(8,128)S(1)}, f32[1,4,32,512]{3,2,1,0:T(8,128)S(1)}, f32[1,4,32,512]{3,2,1,0:T(8,128)S(1)}, f32[1,4,32,512]{3,2,1,0:T(8,128)S(1)}) fusion(f32[8,4,32,512]{3,2,1,0:T(8,128)} %all-gather.2.cloned.1.call-done, s32[]{:T(128)S(6)} %select_n.79, s32[]{:T(128)S(6)} %select_n.85, s32[]{:T(128)S(6)} %select_n.83, ...), kind=kLoop, calls=%fused_computation.20 | loop fusion | bytes 2097168 | tf_op jit(solution)/shard_map/jit(dynamic_index_in_dim)/dynamic_slice | solution.py:217
  75.8 1.1 %pad_maximum_fusion = f32[4,4,32,512]{3,2,1,0:T(8,128)} fusion(f32[1,4,32,512]{3,2,1,0:T(8,128)S(1)} %get-tuple-element.3, f32[1,4,32,512]{3,2,1,0:T(8,128)S(1)} %get-tuple-element.4, f32[1,4,32,512]{3,2,1,0:T(8,128)S(1)} %get-tuple-element.5, f32[1,4,32,512]{3,2,1,0:T(8,128)S(1)} %get-tuple-element.2), kind=kLoop, calls=%fused_computation.3 | loop fusion | flops 786432 | bytes 2097152 | tf_op jit(solution)/shard_map/stack | solution.py:217
  76.9 0.0 all-to-all-done.1
  76.9 4.3 %all-to-all-start = ((f32[4,4,32,512]{3,2,1,0:T(8,128)}), f32[4,4,32,512]{3,2,1,0:T(8,128)S(1)}, u32[]{:S(2)}, u32[]{:S(2)}) async-start(f32[4,4,32,512]{3,2,1,0:T(8,128)} %pad_maximum_fusion), calls=%async_computation | async-start | bytes 2097152 | tf_op jit(solution)/shard_map/all_to_all | solution.py:219
  81.1 0.6 dynamic_slice.27
  84.4 1.0 %reduce.1 = f32[512]{0:T(512)S(1)} reduce(f32[512,1,1]{2,1,0:T(1,128)S(1)} %all-to-all-done.1, f32[]{:T(128)} %constant.101), dimensions={1,2}, to_apply=%all_to_all.8.reduce_sub_computation | reduce | bytes 4100 | tf_op jit(solution)/shard_map/all_to_all | solution.py:200
  85.4 0.1 reshape.67
  85.5 0.1 reduce_sum.28
  85.6 0.7 gather_fusion.2
  86.3 0.6 reduce_max.9
  86.9 1.2 %exponential_reduce_fusion = f32[]{:T(128)} fusion(f32[32]{0:T(128)S(1)} %gather_fusion.2, f32[]{:T(128)} %reduce_max.9), kind=kLoop, calls=%fused_computation.22 | loop fusion | flops 63 | bytes 136 | tf_op jit(solution)/shard_map/reduce_sum | solution.py:232
  89.5 0.6 dynamic_slice.29
  90.1 3.5 %all-to-all-done = f32[4,4,32,512]{3,2,1,0:T(8,128)S(1)} async-done(((f32[4,4,32,512]{3,2,1,0:T(8,128)}), f32[4,4,32,512]{3,2,1,0:T(8,128)S(1)}, u32[]{:S(2)}, u32[]{:S(2)}) %all-to-all-start) | async-done | bytes 1048608 | tf_op jit(solution)/shard_map/all_to_all | solution.py:219
  93.6 0.7 constant_dynamic-slice_fusion
  (8 shorter events, 0.1 us)
Async XLA Ops:
  7.2 12.4 %copy-start = (s32[32]{0:T(128)S(1)}, s32[32]{0:T(128)}, u32[]{:S(2)}) copy-start(s32[32]{0:T(128)} %param.7) | copy-start | bytes 388
  7.2 21.1 %copy-start.3 = (s32[1,512]{1,0:T(1,128)S(1)}, s32[1,512]{1,0:T(1,128)}, u32[]{:S(2)}) copy-start(s32[1,512]{1,0:T(1,128)} %param.10) | copy-start | bytes 6148
  7.2 67.4 %all-gather.2.cloned.1.call-start = ((), (), s32[]{:S(2)}) async-start(), calls=%async_computation.2 | async-start | bytes 2359296 | tf_op jit(solution)/shard_map/all_gather | solution.py:207
  8.2 24.1 %copy-start.4 = (f32[1,512]{1,0:T(1,128)S(1)}, f32[1,512]{1,0:T(1,128)}, u32[]{:S(2)}) copy-start(f32[1,512]{1,0:T(1,128)} %param.11) | copy-start | bytes 6148
  8.2 5.9 %collective-permute-start = (f32[6,8,512]{2,1,0:T(8,128)S(1)}, f32[6,8,512]{2,1,0:T(8,128)S(1)}, u32[]{:S(2)}, u32[]{:S(2)}) collective-permute-start(f32[6,8,512]{2,1,0:T(8,128)S(1)} %get-tuple-element.7), channel_id=1, source_target_pairs={{0,1},{1,2},{2,3},{3,4},{4,5},{5,6},{6,7},{7,8},{8,9},{9,10},{10,1... | collective-permute-start | bytes 294920 | tf_op jit(solution)/shard_map/ppermute | solution.py:157
  10.1 5.8 %collective-permute-start.1 = (f32[6,8,512]{2,1,0:T(8,128)S(1)}, f32[6,8,512]{2,1,0:T(8,128)S(1)}, u32[]{:S(2)}, u32[]{:S(2)}) collective-permute-start(f32[6,8,512]{2,1,0:T(8,128)S(1)} %get-tuple-element.6), channel_id=1, source_target_pairs={{1,0},{2,1},{3,2},{4,3},{5,4},{6,5},{7,6},{8,7},{9,8},{10,9},{11,1... | collective-permute-start | bytes 294920 | tf_op jit(solution)/shard_map/ppermute | solution.py:158
  14.1 1.8 %copy-start.1 = (f32[6,8,512]{2,1,0:T(8,128)}, f32[6,8,512]{2,1,0:T(8,128)S(1)}, u32[]{:S(2)}) copy-start(f32[6,8,512]{2,1,0:T(8,128)S(1)} %collective-permute-done.above_ref) | copy-start | bytes 294916
  16.0 0.6 copy-start.2
  34.4 42.4 %all-to-all-start.1 = ((f32[512,1,1]{2,1,0:T(1,128)}), f32[512,1,1]{2,1,0:T(1,128)S(1)}, u32[]{:S(2)}, u32[]{:S(2)}) async-start(f32[512,1,1]{2,1,0:T(1,128)} %broadcast_in_dim.22), calls=%async_computation.1 | async-start | bytes 524288 | tf_op jit(solution)/shard_map/all_to_all | solution.py:200
  76.9 16.7 %all-to-all-start = ((f32[4,4,32,512]{3,2,1,0:T(8,128)}), f32[4,4,32,512]{3,2,1,0:T(8,128)S(1)}, u32[]{:S(2)}, u32[]{:S(2)}) async-start(f32[4,4,32,512]{3,2,1,0:T(8,128)} %pad_maximum_fusion), calls=%async_computation | async-start | bytes 2097152 | tf_op jit(solution)/shard_map/all_to_all | solution.py:219
Sparse Core Ops, SparseCore 0:
  19.7 54.8 all-gather.1

commit v5 on v4

--- a/solution.py
+++ b/solution.py
@@ -195,10 +195,13 @@
         slots = jnp.where(jnp.arange(n_dom) == me, partial_value, 0.0)
         by_source = lax.psum(slots, ("dx", "dz", "strip"))
     elif LOGLIK_MODE == "a2a":
-        n_all = n_dom * lax.axis_size("strip")
-        spread = jnp.broadcast_to(partial_value, (n_all, 1))
-        every = lax.all_to_all(spread, ("dx", "dz", "strip"), 0, 0, tiled=True)
-        by_source = jnp.sum(every.reshape(n_dom, -1), axis=1)
+        n_strip = lax.axis_size("strip")
+        spread = jnp.broadcast_to(partial_value, (n_strip, 1))
+        strips = lax.all_to_all(spread, "strip", 0, 0, tiled=True)
+        mine_total = jnp.sum(strips)
+        spread2 = jnp.broadcast_to(mine_total, (n_dom, 1))
+        every = lax.all_to_all(spread2, ("dx", "dz"), 0, 0, tiled=True)
+        by_source = every.reshape(n_dom)
     else:
         slots = jnp.where(jnp.arange(n_dom) == me, partial_value, 0.0)
         by_source = butterfly_sum(slots, (("strip", lax.axis_size("strip")), ("dx", nx), ("dz", nz)))

time: 102 us -> 100 us (0.980)
  the two profiles are of different devices: /device:TPU:8 before, /device:TPU:2 now
where the time goes in v5:
time: 100 us; the launch traced here: 99.8 us
  starting transfers between devices  31.7 us (32%)
  between operations  26.4 us (26%)
  waiting for transfers between devices  21.6 us (22%)
  local copies, waits for them, and re-layouts  11.7 us (12%)
  other arithmetic  5.46 us (5%)
  Pallas kernels  2.92 us (3%)
    all_to_all x1, starting transfers between devices, local(): every = lax.all_to_all(spread2, ('dx', 'dz'), 0, 0, tiled=True)  13.5 us
    all_to_all x1, starting transfers between devices, local(): strips = lax.all_to_all(spread, 'strip', 0, 0, tiled=True)  10.2 us
    all_to_all x1, waiting for transfers between devices, local(): strips = lax.all_to_all(spread, 'strip', 0, 0, tiled=True)  7.6 us
    all_to_all x1, starting transfers between devices, local(): moved = lax.all_to_all(picks, 'dx', 0, 0, tiled=False)  4.86 us
    all_to_all x1, waiting for transfers between devices, local(): moved = lax.all_to_all(picks, 'dx', 0, 0, tiled=False)  4.49 us
    all_gather x1, waiting for transfers between devices, local(): along_z = lax.all_gather(fore[0], 'dz', axis=0, tiled=False)  4 us
    ppermute x1, waiting for transfers between devices, forecast_of(): lax.ppermute(packed[:, :margin], 'strip', [(i + 1, i) for i in range(ends)])  3.23 us
    gather x1, local copies, waits for them, and re-layouts, local(): seen = jnp.take(eta, obs_cells[0], axis=0)  3.14 us
  transfers between devices with their start and end apart: 6, of which 5 were waited for; matrix products, arithmetic and copies ran while one was open for 15% of the time, Pallas kernels for 0%

profile of v5, /device:TPU:2, one launch (start us, length us, event | category | flops | bytes accessed | tf_op | source)
XLA Modules:
  0.0 99.8 jit_solution(3013063648583036348)
XLA Ops:
  7.2 0.0 copy-start
  7.2 0.0 copy-start.3
  7.2 0.0 all-gather.2.cloned.1.call-start
  7.2 1.0 pad_maximum_fusion.1
  8.2 0.0 copy-start.4
  8.2 1.7 %collective-permute-start = (f32[6,8,512]{2,1,0:T(8,128)S(1)}, f32[6,8,512]{2,1,0:T(8,128)S(1)}, u32[]{:S(2)}, u32[]{:S(2)}) collective-permute-start(f32[6,8,512]{2,1,0:T(8,128)S(1)} %get-tuple-element.7), channel_id=1, source_target_pairs={{0,1},{1,2},{2,3},{3,4},{4,5},{5,6},{6,7},{7,8},{8,9},{9,10},{10,1... | collective-permute-start | bytes 294920 | tf_op jit(solution)/shard_map/ppermute | solution.py:157
  10.0 1.3 %collective-permute-start.1 = (f32[6,8,512]{2,1,0:T(8,128)S(1)}, f32[6,8,512]{2,1,0:T(8,128)S(1)}, u32[]{:S(2)}, u32[]{:S(2)}) collective-permute-start(f32[6,8,512]{2,1,0:T(8,128)S(1)} %get-tuple-element.6), channel_id=1, source_target_pairs={{1,0},{2,1},{3,2},{4,3},{5,4},{6,5},{7,6},{8,7},{9,8},{10,9},{11,1... | collective-permute-start | bytes 294920 | tf_op jit(solution)/shard_map/ppermute | solution.py:158
  11.3 0.0 collective-permute-done.above_ref
  11.3 0.0 copy-start.1
  11.3 3.2 %collective-permute-done.1.below_ref = f32[6,8,512]{2,1,0:T(8,128)S(1)} collective-permute-done((f32[6,8,512]{2,1,0:T(8,128)S(1)}, f32[6,8,512]{2,1,0:T(8,128)S(1)}, u32[]{:S(2)}, u32[]{:S(2)}) %collective-permute-start.1) | collective-permute-done | bytes 98336 | tf_op jit(solution)/shard_map/ppermute | solution.py:158
  14.5 0.0 copy-start.2
  14.5 0.0 copy-done.1
  14.5 0.6 copy-done.2
  15.1 2.9 %shard_map.77 = f32[1,4,32,512]{3,2,1,0:T(8,128)} custom-call(s32[1]{0:T(128)} %bitcast.base_ref, f32[4,32,512]{2,1,0:T(8,128)} %bitcast.21, f32[32,512]{1,0:T(8,128)} %deep_ref.1, f32[32,512]{1,0:T(8,128)} %drag_ref.1, f32[6,8,512]{2,1,0:T(8,128)} %copy-done.1, f32[6,8,512]{2,1,0:T(8,128)} %copy-done.2), custom_call_target="tpu_custom_call" | custom-call | tf_op jit(solution)/shard_map/pallas_call | solution.py:162
  18.1 0.0 all-gather.2.cloned.1.call-update
  18.1 0.0 copy-done
  18.1 0.6 gather_fusion
  18.8 0.7 fusion.1
  27.0 0.0 copy-done.3
  27.1 0.8 slice_bitcast_fusion
  27.9 3.1 %gather_fusion.1 = f32[512]{0:T(512)S(1)} fusion(f32[16384]{0:T(1024)S(1)} %bitcast.19, s32[1024]{0:T(1024)S(1)} %pad_clamp_fusion.1), kind=kCustom, calls=%fused_computation.1 | custom fusion | bytes 6144 | tf_op jit(solution)/shard_map/jit(_take)/gather | solution.py:191
  31.1 0.0 copy-done.4
  31.1 0.6 multiply_reduce_fusion
  32.4 0.6 broadcast_in_dim.25
  32.9 10.2 %all-to-all-start.1 = ((f32[16,1,1]{2,1,0:T(1,128)}), f32[16,1,1]{2,1,0:T(1,128)S(1)}, u32[]{:S(2)}, u32[]{:S(2)}) async-start(f32[16,1,1]{2,1,0:T(1,128)} %broadcast_in_dim.25), calls=%async_computation.1 | async-start | bytes 16384 | tf_op jit(solution)/shard_map/all_to_all | solution.py:200
  43.2 7.6 %all-to-all-done.1 = f32[16,1,1]{2,1,0:T(1,128)S(1)} async-done(((f32[16,1,1]{2,1,0:T(1,128)}), f32[16,1,1]{2,1,0:T(1,128)S(1)}, u32[]{:S(2)}, u32[]{:S(2)}) %all-to-all-start.1) | async-done | bytes 96 | tf_op jit(solution)/shard_map/all_to_all | solution.py:200
  50.8 0.6 reduce_sum.28
  51.4 1.3 %broadcast_in_dim.26 = f32[32,1,1]{2,1,0:T(1,128)} broadcast(f32[]{:T(128)} %reduce_sum.28), dimensions={} | broadcast | bytes 132 | tf_op jit(solution)/shard_map/broadcast_in_dim | solution.py:202
  52.7 13.5 %all-to-all-start.2 = ((f32[32,1,1]{2,1,0:T(1,128)}), f32[32,1,1]{2,1,0:T(1,128)S(1)}, u32[]{:S(2)}, u32[]{:S(2)}) async-start(f32[32,1,1]{2,1,0:T(1,128)} %broadcast_in_dim.26), calls=%async_computation.2 | async-start | bytes 32768 | tf_op jit(solution)/shard_map/all_to_all | solution.py:203
  66.2 4.0 %all-gather.2.cloned.1.call-done = f32[8,4,32,512]{3,2,1,0:T(8,128)} async-done(((f32[1,4,32,512]{3,2,1,0:T(8,128)}), f32[8,4,32,512]{3,2,1,0:T(8,128)}) %all-gather.2.cloned.1.call-update) | async-done | bytes 2097168 | tf_op jit(solution)/shard_map/all_gather | solution.py:210
  70.2 1.3 %constant_dynamic-slice_fusion.4 = (f32[1,4,32,512]{3,2,1,0:T(8,128)S(1)}, f32[1,4,32,512]{3,2,1,0:T(8,128)S(1)}, f32[1,4,32,512]{3,2,1,0:T(8,128)S(1)}, f32[1,4,32,512]{3,2,1,0:T(8,128)S(1)}) fusion(f32[8,4,32,512]{3,2,1,0:T(8,128)} %all-gather.2.cloned.1.call-done, s32[]{:T(128)S(6)} %select_n.79, s32[]{:T(128)S(6)} %select_n.85, s32[]{:T(128)S(6)} %select_n.83, ...), kind=kLoop, calls=%fused_computation.20 | loop fusion | bytes 2097168 | tf_op jit(solution)/shard_map/jit(dynamic_index_in_dim)/dynamic_slice | solution.py:220
  71.4 1.1 %pad_maximum_fusion = f32[4,4,32,512]{3,2,1,0:T(8,128)} fusion(f32[1,4,32,512]{3,2,1,0:T(8,128)S(1)} %get-tuple-element.3, f32[1,4,32,512]{3,2,1,0:T(8,128)S(1)} %get-tuple-element.4, f32[1,4,32,512]{3,2,1,0:T(8,128)S(1)} %get-tuple-element.5, f32[1,4,32,512]{3,2,1,0:T(8,128)S(1)} %get-tuple-element.2), kind=kLoop, calls=%fused_computation.3 | loop fusion | flops 786432 | bytes 2097152 | tf_op jit(solution)/shard_map/stack | solution.py:220
  72.5 2.3 %all-to-all-done.2 = f32[32,1,1]{2,1,0:T(1,128)S(1)} async-done(((f32[32,1,1]{2,1,0:T(1,128)}), f32[32,1,1]{2,1,0:T(1,128)S(1)}, u32[]{:S(2)}, u32[]{:S(2)}) %all-to-all-start.2) | async-done | bytes 160 | tf_op jit(solution)/shard_map/all_to_all | solution.py:203
  74.8 4.9 %all-to-all-start = ((f32[4,4,32,512]{3,2,1,0:T(8,128)}), f32[4,4,32,512]{3,2,1,0:T(8,128)S(1)}, u32[]{:S(2)}, u32[]{:S(2)}) async-start(f32[4,4,32,512]{3,2,1,0:T(8,128)} %pad_maximum_fusion), calls=%async_computation | async-start | bytes 2097152 | tf_op jit(solution)/shard_map/all_to_all | solution.py:222
  79.7 0.6 dynamic_slice.27
  82.9 0.3 reduce.3
  83.2 0.7 gather_fusion.2
  83.9 0.6 reduce_max.9
  84.5 1.2 %exponential_reduce_fusion = f32[]{:T(128)} fusion(f32[32]{0:T(128)S(1)} %gather_fusion.2, f32[]{:T(128)} %reduce_max.9), kind=kLoop, calls=%fused_computation.22 | loop fusion | flops 63 | bytes 136 | tf_op jit(solution)/shard_map/reduce_sum | solution.py:235
  87.1 0.6 dynamic_slice.29
  87.7 4.5 %all-to-all-done = f32[4,4,32,512]{3,2,1,0:T(8,128)S(1)} async-done(((f32[4,4,32,512]{3,2,1,0:T(8,128)}), f32[4,4,32,512]{3,2,1,0:T(8,128)S(1)}, u32[]{:S(2)}, u32[]{:S(2)}) %all-to-all-start) | async-done | bytes 1048608 | tf_op jit(solution)/shard_map/all_to_all | solution.py:222
  92.2 0.7 constant_dynamic-slice_fusion
  (8 shorter events, 0.1 us)
Async XLA Ops:
  7.2 11.0 %copy-start = (s32[32]{0:T(128)S(1)}, s32[32]{0:T(128)}, u32[]{:S(2)}) copy-start(s32[32]{0:T(128)} %param.7) | copy-start | bytes 388
  7.2 19.9 %copy-start.3 = (s32[1,512]{1,0:T(1,128)S(1)}, s32[1,512]{1,0:T(1,128)}, u32[]{:S(2)}) copy-start(s32[1,512]{1,0:T(1,128)} %param.10) | copy-start | bytes 6148
  7.2 63.0 %all-gather.2.cloned.1.call-start = ((), (), s32[]{:S(2)}) async-start(), calls=%async_computation.3 | async-start | bytes 2359296 | tf_op jit(solution)/shard_map/all_gather | solution.py:210
  8.2 22.9 %copy-start.4 = (f32[1,512]{1,0:T(1,128)S(1)}, f32[1,512]{1,0:T(1,128)}, u32[]{:S(2)}) copy-start(f32[1,512]{1,0:T(1,128)} %param.11) | copy-start | bytes 6148
  8.2 3.1 %collective-permute-start = (f32[6,8,512]{2,1,0:T(8,128)S(1)}, f32[6,8,512]{2,1,0:T(8,128)S(1)}, u32[]{:S(2)}, u32[]{:S(2)}) collective-permute-start(f32[6,8,512]{2,1,0:T(8,128)S(1)} %get-tuple-element.7), channel_id=1, source_target_pairs={{0,1},{1,2},{2,3},{3,4},{4,5},{5,6},{6,7},{7,8},{8,9},{9,10},{10,1... | collective-permute-start | bytes 294920 | tf_op jit(solution)/shard_map/ppermute | solution.py:157
  10.0 4.6 %collective-permute-start.1 = (f32[6,8,512]{2,1,0:T(8,128)S(1)}, f32[6,8,512]{2,1,0:T(8,128)S(1)}, u32[]{:S(2)}, u32[]{:S(2)}) collective-permute-start(f32[6,8,512]{2,1,0:T(8,128)S(1)} %get-tuple-element.6), channel_id=1, source_target_pairs={{1,0},{2,1},{3,2},{4,3},{5,4},{6,5},{7,6},{8,7},{9,8},{10,9},{11,1... | collective-permute-start | bytes 294920 | tf_op jit(solution)/shard_map/ppermute | solution.py:158
  11.3 3.2 %copy-start.1 = (f32[6,8,512]{2,1,0:T(8,128)}, f32[6,8,512]{2,1,0:T(8,128)S(1)}, u32[]{:S(2)}) copy-start(f32[6,8,512]{2,1,0:T(8,128)S(1)} %collective-permute-done.above_ref) | copy-start | bytes 294916
  14.5 0.6 copy-start.2
  32.9 17.9 %all-to-all-start.1 = ((f32[16,1,1]{2,1,0:T(1,128)}), f32[16,1,1]{2,1,0:T(1,128)S(1)}, u32[]{:S(2)}, u32[]{:S(2)}) async-start(f32[16,1,1]{2,1,0:T(1,128)} %broadcast_in_dim.25), calls=%async_computation.1 | async-start | bytes 16384 | tf_op jit(solution)/shard_map/all_to_all | solution.py:200
  52.7 22.1 %all-to-all-start.2 = ((f32[32,1,1]{2,1,0:T(1,128)}), f32[32,1,1]{2,1,0:T(1,128)S(1)}, u32[]{:S(2)}, u32[]{:S(2)}) async-start(f32[32,1,1]{2,1,0:T(1,128)} %broadcast_in_dim.26), calls=%async_computation.2 | async-start | bytes 32768 | tf_op jit(solution)/shard_map/all_to_all | solution.py:203
  74.8 17.4 %all-to-all-start = ((f32[4,4,32,512]{3,2,1,0:T(8,128)}), f32[4,4,32,512]{3,2,1,0:T(8,128)S(1)}, u32[]{:S(2)}, u32[]{:S(2)}) async-start(f32[4,4,32,512]{3,2,1,0:T(8,128)} %pad_maximum_fusion), calls=%async_computation | async-start | bytes 2097152 | tf_op jit(solution)/shard_map/all_to_all | solution.py:222
Sparse Core Ops, SparseCore 0:
  18.2 51.8 all-gather.1
